TPU v7x, 128 devices: a whole 4x4x4 slice. The times are simulated.
128 devices in a mesh: wide: 16 (over y_hi, z, core), blk: 8 (over x, y_lo).
Axes of the slice: x: 4, y: 4 (y_hi: 2, y_lo: 2; y = y_hi * 2 + y_lo), z: 4, core: 2. Of those that a mesh axis runs over, the one named last changes fastest.
Arguments:
- queries: bfloat16 [512, 64, 512], P(('wide', 'blk')), may hold values from -6 to 6
- references: bfloat16 [256, 64, 512], P(('wide', 'blk')), may hold values from -6 to 6
- query_taps: bfloat16 [16, 9], replicated, may hold values from -2 to 2
- ref_taps: bfloat16 [16, 9], replicated, may hold values from -0.5 to 0.5
- tap_bias: float32 [16], replicated, may hold values from -3 to 3
- candidates: int32 [128, 16], P(('wide', 'blk')), may hold values 0 or 1
Outputs:
- scores: float32 [512, 256], P(('wide', 'blk'))
All inputs are finite; a program needn't handle non-finite values. No bound on the sum of `candidates` on one device may be relied on, other than what follows from the above.
Results may differ from a plain program's by a relative error of at most 0.0006.
Values may be sent and summed in bfloat16 or wider, within the bound.
No kernel may reach another device: no remote copies, remote signals or barrier semaphores. Data moves between devices by JAX's collectives and lax.ppermute only.
A program may use at most 64 MiB of HBM per device.

v0:
```python
import math

import jax
import jax.numpy as jnp
from jax import lax
from jax.sharding import PartitionSpec as P

SIDE = 8


epsilon = 1e-06


def from_behind(x, axis, by):
    length = lax.axis_size(axis)
    return lax.ppermute(x, axis, [(i, (i + by) % length) for i in range(length)])


def conv_table(weights, width):
    count = width * width
    position = jnp.arange(count, dtype=jnp.int32)
    grid_row = position // width
    grid_col = position % width
    delta_row = grid_row[None, :] - grid_row[:, None]
    delta_col = grid_col[None, :] - grid_col[:, None]
    inside = (jnp.abs(delta_row) <= 1) & (jnp.abs(delta_col) <= 1)
    tap_index = (delta_row + 1) * 3 + (delta_col + 1)
    selector = (tap_index[None] == jnp.arange(9, dtype=jnp.int32)[:, None, None]) & inside[None]
    table = jnp.sum(
        jnp.where(selector[None], weights.astype(jnp.float32)[:, :, None, None], jnp.float32(0.0)),
        axis=1,
    )
    return table.astype(jnp.bfloat16)


def normalize(features):
    values = features.astype(jnp.float32)
    inverse_rms = lax.rsqrt(jnp.mean(values * values, axis=-1, keepdims=True) + epsilon)
    return (values * inverse_rms).astype(jnp.bfloat16)


def pair_scores(query_unit, ref_unit, query_table, ref_table, tap_bias):
    count = query_unit.shape[0]
    others = ref_unit.shape[0]
    cell_count = query_unit.shape[1]
    depth = query_unit.shape[2]
    correlation = jnp.einsum(
        "ic,jc->ij",
        query_unit.reshape(count * cell_count, depth),
        ref_unit.reshape(others * cell_count, depth),
        preferred_element_type=jnp.float32,
    )
    correlation = (
        (correlation / math.sqrt(depth))
        .astype(jnp.bfloat16)
        .reshape(count, cell_count, others, cell_count)
    )
    hidden = jnp.einsum(
        "kai,pirj->pkarj", query_table, correlation, preferred_element_type=jnp.float32
    )
    hidden = jnp.maximum(hidden + tap_bias[None, :, None, None, None], 0.0).astype(jnp.bfloat16)
    filtered = jnp.einsum("pkarj,kbj->parb", hidden, ref_table, preferred_element_type=jnp.float32)
    row_pool = jnp.mean(jnp.max(filtered, axis=3), axis=1)
    col_pool = jnp.mean(jnp.max(filtered, axis=1), axis=2)
    return 0.5 * (row_pool + col_pool)


def shards(queries, references, query_taps, ref_taps, tap_bias, candidates):
    query_table = conv_table(query_taps, SIDE)
    ref_table = conv_table(ref_taps, SIDE)
    query_unit = normalize(queries)
    ref_unit = normalize(references)
    cycle_size = lax.axis_size("wide")
    chosen = candidates[0]
    local_rows = query_unit.shape[0]
    carried = lax.all_gather(ref_unit, "blk", axis=0, tiled=True)
    block_rows = carried.shape[0]

    def visit(scores, current, counter):
        anchor = (lax.axis_index("wide") - counter) % cycle_size
        values = lax.cond(
            chosen[anchor] != 0,
            lambda: pair_scores(query_unit, current, query_table, ref_table, tap_bias),
            lambda: jnp.zeros((local_rows, block_rows), jnp.float32),
        )
        return lax.dynamic_update_slice(scores, values, (jnp.int32(0), anchor * block_rows))

    def advance(counter, state):
        scores, current = state
        scores = visit(scores, current, counter)
        return (scores, from_behind(current, "wide", 1))

    start_scores = jnp.zeros((local_rows, cycle_size * block_rows), jnp.float32)
    scores, carried = lax.fori_loop(0, cycle_size - 1, advance, (start_scores, carried))
    scores = visit(scores, carried, jnp.int32(cycle_size - 1))
    return scores


def solution(mesh):
    placed = (
        P(("wide", "blk"), None, None),
        P(("wide", "blk"), None, None),
        P(),
        P(),
        P(),
        P(("wide", "blk"), None),
    )
    return jax.shard_map(
        shards, mesh=mesh, in_specs=placed, out_specs=P(("wide", "blk"), None), check_vma=False
    )
```

profile of v0, /device:TPU:0, one launch (start us, length us, event | category | flops | bytes accessed | tf_op | source)
XLA Modules:
  0.0 394.5 jit_solution(15191075185623106522)
XLA Ops:
  15.4 35.2 %all-gather.2.cloned.1.call-done = bf16[16,64,512]{2,1,0:T(8,128)(2,1)} async-done(((bf16[2,64,512]{2,1,0:T(8,128)(2,1)}), bf16[16,64,512]{2,1,0:T(8,128)(2,1)}) %all-gather.2.cloned.1.call-update) | async-done | bytes 1048592 | tf_op jit(solution)/shard_map/all_gather | solution.py:76
  50.6 320.9 %while.17 = (s32[]{:T(128)}, f32[4,256]{1,0:T(4,128)S(1)}, bf16[16,64,512]{2,1,0:T(8,128)(2,1)}, s32[16]{0:T(128)S(1)}, bf16[4,64,512]{2,1,0:T(8,128)(2,1)S(1)},...) while((s32[]{:T(128)}, f32[4,256]{1,0:T(4,128)S(1)}, ...), condition=%wide.region_11.12_spmd, body=%wide.region_4.11_spmd.sunk | while | flops 1355808896 | bytes 14223704 | solution.py:94
  50.6 2.3 copy.43
  54.5 16.5 %collective-permute-done = bf16[16,64,512]{2,1,0:T(8,128)(2,1)S(1)} collective-permute-done((bf16[16,64,512]{2,1,0:T(8,128)(2,1)}, bf16[16,64,512]{2,1,0:T(8,128)(2,1)S(1)}, u32[]{:S(2)}, u32[]{:S(2)}) %collective-permute-start) | collective-permute-done | bytes 1048608 | tf_op jit(solution)/shard_map/while/body/eval_jaxpr/ppermute | solution.py:16
  72.0 2.3 copy.43
  76.0 16.4 %collective-permute-done = bf16[16,64,512]{2,1,0:T(8,128)(2,1)S(1)} collective-permute-done((bf16[16,64,512]{2,1,0:T(8,128)(2,1)}, bf16[16,64,512]{2,1,0:T(8,128)(2,1)S(1)}, u32[]{:S(2)}, u32[]{:S(2)}) %collective-permute-start) | collective-permute-done | bytes 1048608 | tf_op jit(solution)/shard_map/while/body/eval_jaxpr/ppermute | solution.py:16
  93.4 2.3 copy.43
  97.3 16.4 %collective-permute-done = bf16[16,64,512]{2,1,0:T(8,128)(2,1)S(1)} collective-permute-done((bf16[16,64,512]{2,1,0:T(8,128)(2,1)}, bf16[16,64,512]{2,1,0:T(8,128)(2,1)S(1)}, u32[]{:S(2)}, u32[]{:S(2)}) %collective-permute-start) | collective-permute-done | bytes 1048608 | tf_op jit(solution)/shard_map/while/body/eval_jaxpr/ppermute | solution.py:16
  114.8 2.3 copy.43
  118.4 14.2 %conditional.4 = (f32[4,16]{1,0:T(4,128)S(1)}) conditional(s32[]{:T(128)} %bitcast.62, () %tuple.56, (bf16[4,64,512]{2,1,0:T(8,128)(2,1)S(1)}, bf16[16,64,512]{2,1,0:T(8,128)(2,1)}, bf16[16,64,64]{2,1,0:T(8,128)(2,1)S(1)}, f32[16]{0:T(128)S(1)}, bf16[16,64,64]{2,1,0:T(8,128)(2,1)S(1)}) %tuple.57), branch_computations={%region_5.5_spmd, %region_6.10_spmd} | conditional | flops 1355808896 | bytes 3736912 | solution.py:81
  118.5 1.7 fusion.7
  120.8 11.6 %bitcast_reduce_fusion = (f32[4,16,64]{2,1,0:T(8,128)S(1)}, f32[4,64,16]{1,2,0:T(8,128)S(1)}) fusion(bf16[16,64,64]{2,1,0:T(8,128)(2,1)S(1)} %get-tuple-element.231, f32[16]{0:T(128)S(1)} %get-tuple-element.230, bf16[4,64,16,64,1]{3,2,1,0,4:T(8,128)(2,1)S(1)} %bitcast.64, bf16[16,64,64]{2,1,0:T(8,128)(2,1)S(1)} %get-tuple-element.229), kind=kOutput, calls=%fused_computation.6 | convolution fusion | flops 1086840832 | bytes 819264 | tf_op jit(solution)/shard_map/while/body/eval_jaxpr/cond/branch_1_fun/pkarj,kbj->parb/dot_general | solution.py:62
  132.9 2.2 collective-permute-done
  136.2 2.3 copy.43
  139.8 14.2 %conditional.4 = (f32[4,16]{1,0:T(4,128)S(1)}) conditional(s32[]{:T(128)} %bitcast.62, () %tuple.56, (bf16[4,64,512]{2,1,0:T(8,128)(2,1)S(1)}, bf16[16,64,512]{2,1,0:T(8,128)(2,1)}, bf16[16,64,64]{2,1,0:T(8,128)(2,1)S(1)}, f32[16]{0:T(128)S(1)}, bf16[16,64,64]{2,1,0:T(8,128)(2,1)S(1)}) %tuple.57), branch_computations={%region_5.5_spmd, %region_6.10_spmd} | conditional | flops 1355808896 | bytes 3736912 | solution.py:81
  139.9 1.7 fusion.7
  142.2 11.6 %bitcast_reduce_fusion = (f32[4,16,64]{2,1,0:T(8,128)S(1)}, f32[4,64,16]{1,2,0:T(8,128)S(1)}) fusion(bf16[16,64,64]{2,1,0:T(8,128)(2,1)S(1)} %get-tuple-element.231, f32[16]{0:T(128)S(1)} %get-tuple-element.230, bf16[4,64,16,64,1]{3,2,1,0,4:T(8,128)(2,1)S(1)} %bitcast.64, bf16[16,64,64]{2,1,0:T(8,128)(2,1)S(1)} %get-tuple-element.229), kind=kOutput, calls=%fused_computation.6 | convolution fusion | flops 1086840832 | bytes 819264 | tf_op jit(solution)/shard_map/while/body/eval_jaxpr/cond/branch_1_fun/pkarj,kbj->parb/dot_general | solution.py:62
  154.3 2.2 collective-permute-done
  157.6 2.3 copy.43
  161.5 16.4 %collective-permute-done = bf16[16,64,512]{2,1,0:T(8,128)(2,1)S(1)} collective-permute-done((bf16[16,64,512]{2,1,0:T(8,128)(2,1)}, bf16[16,64,512]{2,1,0:T(8,128)(2,1)S(1)}, u32[]{:S(2)}, u32[]{:S(2)}) %collective-permute-start) | collective-permute-done | bytes 1048608 | tf_op jit(solution)/shard_map/while/body/eval_jaxpr/ppermute | solution.py:16
  178.9 2.3 copy.43
  182.6 14.2 %conditional.4 = (f32[4,16]{1,0:T(4,128)S(1)}) conditional(s32[]{:T(128)} %bitcast.62, () %tuple.56, (bf16[4,64,512]{2,1,0:T(8,128)(2,1)S(1)}, bf16[16,64,512]{2,1,0:T(8,128)(2,1)}, bf16[16,64,64]{2,1,0:T(8,128)(2,1)S(1)}, f32[16]{0:T(128)S(1)}, bf16[16,64,64]{2,1,0:T(8,128)(2,1)S(1)}) %tuple.57), branch_computations={%region_5.5_spmd, %region_6.10_spmd} | conditional | flops 1355808896 | bytes 3736912 | solution.py:81
  185.0 11.6 %bitcast_reduce_fusion = (f32[4,16,64]{2,1,0:T(8,128)S(1)}, f32[4,64,16]{1,2,0:T(8,128)S(1)}) fusion(bf16[16,64,64]{2,1,0:T(8,128)(2,1)S(1)} %get-tuple-element.231, f32[16]{0:T(128)S(1)} %get-tuple-element.230, bf16[4,64,16,64,1]{3,2,1,0,4:T(8,128)(2,1)S(1)} %bitcast.64, bf16[16,64,64]{2,1,0:T(8,128)(2,1)S(1)} %get-tuple-element.229), kind=kOutput, calls=%fused_computation.6 | convolution fusion | flops 1086840832 | bytes 819264 | tf_op jit(solution)/shard_map/while/body/eval_jaxpr/cond/branch_1_fun/pkarj,kbj->parb/dot_general | solution.py:62
  197.1 2.2 collective-permute-done
  200.3 2.3 copy.43
  204.3 16.4 %collective-permute-done = bf16[16,64,512]{2,1,0:T(8,128)(2,1)S(1)} collective-permute-done((bf16[16,64,512]{2,1,0:T(8,128)(2,1)}, bf16[16,64,512]{2,1,0:T(8,128)(2,1)S(1)}, u32[]{:S(2)}, u32[]{:S(2)}) %collective-permute-start) | collective-permute-done | bytes 1048608 | tf_op jit(solution)/shard_map/while/body/eval_jaxpr/ppermute | solution.py:16
  221.7 2.3 copy.43
  225.6 16.5 %collective-permute-done = bf16[16,64,512]{2,1,0:T(8,128)(2,1)S(1)} collective-permute-done((bf16[16,64,512]{2,1,0:T(8,128)(2,1)}, bf16[16,64,512]{2,1,0:T(8,128)(2,1)S(1)}, u32[]{:S(2)}, u32[]{:S(2)}) %collective-permute-start) | collective-permute-done | bytes 1048608 | tf_op jit(solution)/shard_map/while/body/eval_jaxpr/ppermute | solution.py:16
  243.1 2.3 copy.43
  247.1 16.4 %collective-permute-done = bf16[16,64,512]{2,1,0:T(8,128)(2,1)S(1)} collective-permute-done((bf16[16,64,512]{2,1,0:T(8,128)(2,1)}, bf16[16,64,512]{2,1,0:T(8,128)(2,1)S(1)}, u32[]{:S(2)}, u32[]{:S(2)}) %collective-permute-start) | collective-permute-done | bytes 1048608 | tf_op jit(solution)/shard_map/while/body/eval_jaxpr/ppermute | solution.py:16
  264.5 2.3 copy.43
  268.5 16.4 %collective-permute-done = bf16[16,64,512]{2,1,0:T(8,128)(2,1)S(1)} collective-permute-done((bf16[16,64,512]{2,1,0:T(8,128)(2,1)}, bf16[16,64,512]{2,1,0:T(8,128)(2,1)S(1)}, u32[]{:S(2)}, u32[]{:S(2)}) %collective-permute-start) | collective-permute-done | bytes 1048608 | tf_op jit(solution)/shard_map/while/body/eval_jaxpr/ppermute | solution.py:16
  285.9 2.3 copy.43
  289.9 16.4 %collective-permute-done = bf16[16,64,512]{2,1,0:T(8,128)(2,1)S(1)} collective-permute-done((bf16[16,64,512]{2,1,0:T(8,128)(2,1)}, bf16[16,64,512]{2,1,0:T(8,128)(2,1)S(1)}, u32[]{:S(2)}, u32[]{:S(2)}) %collective-permute-start) | collective-permute-done | bytes 1048608 | tf_op jit(solution)/shard_map/while/body/eval_jaxpr/ppermute | solution.py:16
  307.3 2.3 copy.43
  311.0 14.2 %conditional.4 = (f32[4,16]{1,0:T(4,128)S(1)}) conditional(s32[]{:T(128)} %bitcast.62, () %tuple.56, (bf16[4,64,512]{2,1,0:T(8,128)(2,1)S(1)}, bf16[16,64,512]{2,1,0:T(8,128)(2,1)}, bf16[16,64,64]{2,1,0:T(8,128)(2,1)S(1)}, f32[16]{0:T(128)S(1)}, bf16[16,64,64]{2,1,0:T(8,128)(2,1)S(1)}) %tuple.57), branch_computations={%region_5.5_spmd, %region_6.10_spmd} | conditional | flops 1355808896 | bytes 3736912 | solution.py:81
  311.0 1.7 fusion.7
  313.3 11.6 %bitcast_reduce_fusion = (f32[4,16,64]{2,1,0:T(8,128)S(1)}, f32[4,64,16]{1,2,0:T(8,128)S(1)}) fusion(bf16[16,64,64]{2,1,0:T(8,128)(2,1)S(1)} %get-tuple-element.231, f32[16]{0:T(128)S(1)} %get-tuple-element.230, bf16[4,64,16,64,1]{3,2,1,0,4:T(8,128)(2,1)S(1)} %bitcast.64, bf16[16,64,64]{2,1,0:T(8,128)(2,1)S(1)} %get-tuple-element.229), kind=kOutput, calls=%fused_computation.6 | convolution fusion | flops 1086840832 | bytes 819264 | tf_op jit(solution)/shard_map/while/body/eval_jaxpr/cond/branch_1_fun/pkarj,kbj->parb/dot_general | solution.py:62
  325.4 2.2 collective-permute-done
  328.7 2.3 copy.43
  332.6 16.4 %collective-permute-done = bf16[16,64,512]{2,1,0:T(8,128)(2,1)S(1)} collective-permute-done((bf16[16,64,512]{2,1,0:T(8,128)(2,1)}, bf16[16,64,512]{2,1,0:T(8,128)(2,1)S(1)}, u32[]{:S(2)}, u32[]{:S(2)}) %collective-permute-start) | collective-permute-done | bytes 1048608 | tf_op jit(solution)/shard_map/while/body/eval_jaxpr/ppermute | solution.py:16
  350.1 2.3 copy.43
  353.7 14.2 %conditional.4 = (f32[4,16]{1,0:T(4,128)S(1)}) conditional(s32[]{:T(128)} %bitcast.62, () %tuple.56, (bf16[4,64,512]{2,1,0:T(8,128)(2,1)S(1)}, bf16[16,64,512]{2,1,0:T(8,128)(2,1)}, bf16[16,64,64]{2,1,0:T(8,128)(2,1)S(1)}, f32[16]{0:T(128)S(1)}, bf16[16,64,64]{2,1,0:T(8,128)(2,1)S(1)}) %tuple.57), branch_computations={%region_5.5_spmd, %region_6.10_spmd} | conditional | flops 1355808896 | bytes 3736912 | solution.py:81
  353.8 1.7 fusion.7
  356.1 11.6 %bitcast_reduce_fusion = (f32[4,16,64]{2,1,0:T(8,128)S(1)}, f32[4,64,16]{1,2,0:T(8,128)S(1)}) fusion(bf16[16,64,64]{2,1,0:T(8,128)(2,1)S(1)} %get-tuple-element.231, f32[16]{0:T(128)S(1)} %get-tuple-element.230, bf16[4,64,16,64,1]{3,2,1,0,4:T(8,128)(2,1)S(1)} %bitcast.64, bf16[16,64,64]{2,1,0:T(8,128)(2,1)S(1)} %get-tuple-element.229), kind=kOutput, calls=%fused_computation.6 | convolution fusion | flops 1086840832 | bytes 819264 | tf_op jit(solution)/shard_map/while/body/eval_jaxpr/cond/branch_1_fun/pkarj,kbj->parb/dot_general | solution.py:62
  368.2 2.2 collective-permute-done
  372.1 14.2 %conditional.2 = (f32[4,16]{1,0:T(4,128)S(1)}) conditional(s32[]{:T(128)} %bitcast.22, () %tuple.40, (bf16[4,64,512]{2,1,0:T(8,128)(2,1)S(1)}, bf16[16,64,512]{2,1,0:T(8,128)(2,1)}, bf16[16,64,64]{2,1,0:T(8,128)(2,1)S(1)}, f32[16]{0:T(128)S(1)}, bf16[16,64,64]{2,1,0:T(8,128)(2,1)S(1)}) %tuple.72), branch_computations={%region_12.13_spmd, %region_13.18_spmd} | conditional | flops 1355808896 | bytes 3736912 | solution.py:81
  374.4 11.6 %bitcast_reduce_fusion.2 = (f32[4,16,64]{2,1,0:T(8,128)S(1)}, f32[4,64,16]{1,2,0:T(8,128)S(1)}) fusion(bf16[16,64,64]{2,1,0:T(8,128)(2,1)S(1)} %get-tuple-element.245, f32[16]{0:T(128)S(1)} %get-tuple-element.244, bf16[4,64,16,64,1]{3,2,1,0,4:T(8,128)(2,1)S(1)} %bitcast.67, bf16[16,64,64]{2,1,0:T(8,128)(2,1)S(1)} %get-tuple-element.243), kind=kOutput, calls=%fused_computation.21 | convolution fusion | flops 1086840832 | bytes 819264 | tf_op jit(solution)/shard_map/cond/branch_1_fun/pkarj,kbj->parb/dot_general | solution.py:62
  (147 shorter events, 48.0 us)
Async XLA Ops:
  6.5 7.3 %copy-start.1 = (bf16[4,64,512]{2,1,0:T(8,128)(2,1)S(1)}, bf16[4,64,512]{2,1,0:T(8,128)(2,1)}, u32[]{:S(2)}) copy-start(bf16[4,64,512]{2,1,0:T(8,128)(2,1)} %param.12) | copy-start | bytes 786436
  6.5 44.1 %all-gather.2.cloned.1.call-start = ((), (), s32[]{:S(2)}) async-start(), calls=%async_computation | async-start | bytes 1179648 | tf_op jit(solution)/shard_map/all_gather | solution.py:76
  7.6 43.0 %copy-start.3 = (s32[1,16]{1,0:T(1,128)S(1)}, s32[1,16]{1,0:T(1,128)}, u32[]{:S(2)}) copy-start(s32[1,16]{1,0:T(1,128)} %param.17) | copy-start | bytes 196
  7.6 43.0 %copy-start.4 = (f32[16]{0:T(128)S(1)}, f32[16]{0:T(128)}, u32[]{:S(2)}) copy-start(f32[16]{0:T(128)} %param.16) | copy-start | bytes 196
  52.9 18.0 %collective-permute-start = (bf16[16,64,512]{2,1,0:T(8,128)(2,1)}, bf16[16,64,512]{2,1,0:T(8,128)(2,1)S(1)}, u32[]{:S(2)}, u32[]{:S(2)}) collective-permute-start(bf16[16,64,512]{2,1,0:T(8,128)(2,1)} %copy.43), channel_id=1, source_target_pairs={{0,8},{8,16},{16,24},{24,32},{32,40},{40,48},{48,56},{56,64},{64,7... | collective-permute-start | bytes 3145736 | tf_op jit(solution)/shard_map/while/body/eval_jaxpr/ppermute | solution.py:16
  71.0 1.0 copy-start
  74.3 18.0 %collective-permute-start = (bf16[16,64,512]{2,1,0:T(8,128)(2,1)}, bf16[16,64,512]{2,1,0:T(8,128)(2,1)S(1)}, u32[]{:S(2)}, u32[]{:S(2)}) collective-permute-start(bf16[16,64,512]{2,1,0:T(8,128)(2,1)} %copy.43), channel_id=1, source_target_pairs={{0,8},{8,16},{16,24},{24,32},{32,40},{40,48},{48,56},{56,64},{64,7... | collective-permute-start | bytes 3145736 | tf_op jit(solution)/shard_map/while/body/eval_jaxpr/ppermute | solution.py:16
  92.3 1.0 copy-start
  95.7 18.0 %collective-permute-start = (bf16[16,64,512]{2,1,0:T(8,128)(2,1)}, bf16[16,64,512]{2,1,0:T(8,128)(2,1)S(1)}, u32[]{:S(2)}, u32[]{:S(2)}) collective-permute-start(bf16[16,64,512]{2,1,0:T(8,128)(2,1)} %copy.43), channel_id=1, source_target_pairs={{0,8},{8,16},{16,24},{24,32},{32,40},{40,48},{48,56},{56,64},{64,7... | collective-permute-start | bytes 3145736 | tf_op jit(solution)/shard_map/while/body/eval_jaxpr/ppermute | solution.py:16
  113.7 1.0 copy-start
  117.1 18.0 %collective-permute-start = (bf16[16,64,512]{2,1,0:T(8,128)(2,1)}, bf16[16,64,512]{2,1,0:T(8,128)(2,1)S(1)}, u32[]{:S(2)}, u32[]{:S(2)}) collective-permute-start(bf16[16,64,512]{2,1,0:T(8,128)(2,1)} %copy.43), channel_id=1, source_target_pairs={{0,8},{8,16},{16,24},{24,32},{32,40},{40,48},{48,56},{56,64},{64,7... | collective-permute-start | bytes 3145736 | tf_op jit(solution)/shard_map/while/body/eval_jaxpr/ppermute | solution.py:16
  135.1 1.0 copy-start
  138.5 18.0 %collective-permute-start = (bf16[16,64,512]{2,1,0:T(8,128)(2,1)}, bf16[16,64,512]{2,1,0:T(8,128)(2,1)S(1)}, u32[]{:S(2)}, u32[]{:S(2)}) collective-permute-start(bf16[16,64,512]{2,1,0:T(8,128)(2,1)} %copy.43), channel_id=1, source_target_pairs={{0,8},{8,16},{16,24},{24,32},{32,40},{40,48},{48,56},{56,64},{64,7... | collective-permute-start | bytes 3145736 | tf_op jit(solution)/shard_map/while/body/eval_jaxpr/ppermute | solution.py:16
  156.5 1.0 copy-start
  159.9 18.0 %collective-permute-start = (bf16[16,64,512]{2,1,0:T(8,128)(2,1)}, bf16[16,64,512]{2,1,0:T(8,128)(2,1)S(1)}, u32[]{:S(2)}, u32[]{:S(2)}) collective-permute-start(bf16[16,64,512]{2,1,0:T(8,128)(2,1)} %copy.43), channel_id=1, source_target_pairs={{0,8},{8,16},{16,24},{24,32},{32,40},{40,48},{48,56},{56,64},{64,7... | collective-permute-start | bytes 3145736 | tf_op jit(solution)/shard_map/while/body/eval_jaxpr/ppermute | solution.py:16
  177.9 1.0 copy-start
  181.2 18.0 %collective-permute-start = (bf16[16,64,512]{2,1,0:T(8,128)(2,1)}, bf16[16,64,512]{2,1,0:T(8,128)(2,1)S(1)}, u32[]{:S(2)}, u32[]{:S(2)}) collective-permute-start(bf16[16,64,512]{2,1,0:T(8,128)(2,1)} %copy.43), channel_id=1, source_target_pairs={{0,8},{8,16},{16,24},{24,32},{32,40},{40,48},{48,56},{56,64},{64,7... | collective-permute-start | bytes 3145736 | tf_op jit(solution)/shard_map/while/body/eval_jaxpr/ppermute | solution.py:16
  199.3 1.0 copy-start
  202.6 18.0 %collective-permute-start = (bf16[16,64,512]{2,1,0:T(8,128)(2,1)}, bf16[16,64,512]{2,1,0:T(8,128)(2,1)S(1)}, u32[]{:S(2)}, u32[]{:S(2)}) collective-permute-start(bf16[16,64,512]{2,1,0:T(8,128)(2,1)} %copy.43), channel_id=1, source_target_pairs={{0,8},{8,16},{16,24},{24,32},{32,40},{40,48},{48,56},{56,64},{64,7... | collective-permute-start | bytes 3145736 | tf_op jit(solution)/shard_map/while/body/eval_jaxpr/ppermute | solution.py:16
  220.7 1.0 copy-start
  224.0 18.0 %collective-permute-start = (bf16[16,64,512]{2,1,0:T(8,128)(2,1)}, bf16[16,64,512]{2,1,0:T(8,128)(2,1)S(1)}, u32[]{:S(2)}, u32[]{:S(2)}) collective-permute-start(bf16[16,64,512]{2,1,0:T(8,128)(2,1)} %copy.43), channel_id=1, source_target_pairs={{0,8},{8,16},{16,24},{24,32},{32,40},{40,48},{48,56},{56,64},{64,7... | collective-permute-start | bytes 3145736 | tf_op jit(solution)/shard_map/while/body/eval_jaxpr/ppermute | solution.py:16
  242.1 1.0 copy-start
  245.4 18.0 %collective-permute-start = (bf16[16,64,512]{2,1,0:T(8,128)(2,1)}, bf16[16,64,512]{2,1,0:T(8,128)(2,1)S(1)}, u32[]{:S(2)}, u32[]{:S(2)}) collective-permute-start(bf16[16,64,512]{2,1,0:T(8,128)(2,1)} %copy.43), channel_id=1, source_target_pairs={{0,8},{8,16},{16,24},{24,32},{32,40},{40,48},{48,56},{56,64},{64,7... | collective-permute-start | bytes 3145736 | tf_op jit(solution)/shard_map/while/body/eval_jaxpr/ppermute | solution.py:16
  263.5 1.0 copy-start
  266.8 18.0 %collective-permute-start = (bf16[16,64,512]{2,1,0:T(8,128)(2,1)}, bf16[16,64,512]{2,1,0:T(8,128)(2,1)S(1)}, u32[]{:S(2)}, u32[]{:S(2)}) collective-permute-start(bf16[16,64,512]{2,1,0:T(8,128)(2,1)} %copy.43), channel_id=1, source_target_pairs={{0,8},{8,16},{16,24},{24,32},{32,40},{40,48},{48,56},{56,64},{64,7... | collective-permute-start | bytes 3145736 | tf_op jit(solution)/shard_map/while/body/eval_jaxpr/ppermute | solution.py:16
  284.9 1.0 copy-start
  288.2 18.0 %collective-permute-start = (bf16[16,64,512]{2,1,0:T(8,128)(2,1)}, bf16[16,64,512]{2,1,0:T(8,128)(2,1)S(1)}, u32[]{:S(2)}, u32[]{:S(2)}) collective-permute-start(bf16[16,64,512]{2,1,0:T(8,128)(2,1)} %copy.43), channel_id=1, source_target_pairs={{0,8},{8,16},{16,24},{24,32},{32,40},{40,48},{48,56},{56,64},{64,7... | collective-permute-start | bytes 3145736 | tf_op jit(solution)/shard_map/while/body/eval_jaxpr/ppermute | solution.py:16
  306.2 1.0 copy-start
  309.6 18.0 %collective-permute-start = (bf16[16,64,512]{2,1,0:T(8,128)(2,1)}, bf16[16,64,512]{2,1,0:T(8,128)(2,1)S(1)}, u32[]{:S(2)}, u32[]{:S(2)}) collective-permute-start(bf16[16,64,512]{2,1,0:T(8,128)(2,1)} %copy.43), channel_id=1, source_target_pairs={{0,8},{8,16},{16,24},{24,32},{32,40},{40,48},{48,56},{56,64},{64,7... | collective-permute-start | bytes 3145736 | tf_op jit(solution)/shard_map/while/body/eval_jaxpr/ppermute | solution.py:16
  327.6 1.0 copy-start
  331.0 18.0 %collective-permute-start = (bf16[16,64,512]{2,1,0:T(8,128)(2,1)}, bf16[16,64,512]{2,1,0:T(8,128)(2,1)S(1)}, u32[]{:S(2)}, u32[]{:S(2)}) collective-permute-start(bf16[16,64,512]{2,1,0:T(8,128)(2,1)} %copy.43), channel_id=1, source_target_pairs={{0,8},{8,16},{16,24},{24,32},{32,40},{40,48},{48,56},{56,64},{64,7... | collective-permute-start | bytes 3145736 | tf_op jit(solution)/shard_map/while/body/eval_jaxpr/ppermute | solution.py:16
  349.0 1.0 copy-start
  352.4 18.0 %collective-permute-start = (bf16[16,64,512]{2,1,0:T(8,128)(2,1)}, bf16[16,64,512]{2,1,0:T(8,128)(2,1)S(1)}, u32[]{:S(2)}, u32[]{:S(2)}) collective-permute-start(bf16[16,64,512]{2,1,0:T(8,128)(2,1)} %copy.43), channel_id=1, source_target_pairs={{0,8},{8,16},{16,24},{24,32},{32,40},{40,48},{48,56},{56,64},{64,7... | collective-permute-start | bytes 3145736 | tf_op jit(solution)/shard_map/while/body/eval_jaxpr/ppermute | solution.py:16
  370.4 1.0 copy-start
  371.5 0.6 copy-start.2
Sparse Core Ops, SparseCore 0:
  9.4 41.1 all-gather.1
where the time goes:
time: 396 us; the launch traced here: 395 us
  waiting for transfers between devices  210 us (53%)
  matrix products  80 us (20%)
  local copies, waits for them, and re-layouts  69.7 us (18%)
  between operations  14.1 us (4%)
  loops' own time  11.2 us (3%)
  other arithmetic  9.25 us (2%)
    ppermute x15, waiting for transfers between devices, from_behind(): lax.ppermute(x, axis, [(i, (i + by) % length) for i in range(length)])  175 us
    dot_general x6, matrix products, pair_scores(): jnp.einsum('pkarj,kbj->parb', hidden, ref_table, preferred_element_type=j...  69.8 us
    all_gather x1, waiting for transfers between devices, shards(): carried = lax.all_gather(ref_unit, 'blk', axis=0, tiled=True)  35.2 us
    another operation x25, local copies, waits for them, and re-layouts  34.6 us
    while x30, local copies, waits for them, and re-layouts  15.5 us
    another operation x1, loops' own time, shards(): lax.fori_loop(0, cycle_size - 1, advance, (start_scores, carried))  10.8 us
    dot_general x6, matrix products, pair_scores(): jnp.einsum('ic,jc->ij', query_unit.reshape(count * cell_count, depth), re...  10.2 us
    dynamic_slice x15, local copies, waits for them, and re-layouts, visit(): chosen[anchor] != 0  9.9 us
  transfers between devices with their start and end apart: 16, of which 16 were waited for; matrix products, arithmetic and copies ran while one was open for 23% of the time, Pallas kernels for 0%

commit v1 on v0

v1 whole, which is shorter than its diff:
```python
import math

import jax
import jax.numpy as jnp
from jax import lax
from jax.experimental import pallas as pl
from jax.experimental.pallas import tpu as pltpu
from jax.sharding import PartitionSpec as P

SIDE = 8


epsilon = 1e-06


def conv_table(weights, width):
    count = width * width
    position = jnp.arange(count, dtype=jnp.int32)
    grid_row = position // width
    grid_col = position % width
    delta_row = grid_row[None, :] - grid_row[:, None]
    delta_col = grid_col[None, :] - grid_col[:, None]
    inside = (jnp.abs(delta_row) <= 1) & (jnp.abs(delta_col) <= 1)
    tap_index = (delta_row + 1) * 3 + (delta_col + 1)
    selector = (tap_index[None] == jnp.arange(9, dtype=jnp.int32)[:, None, None]) & inside[None]
    table = jnp.sum(
        jnp.where(selector[None], weights.astype(jnp.float32)[:, :, None, None], jnp.float32(0.0)),
        axis=1,
    )
    return table.astype(jnp.bfloat16)


def normalize(features):
    values = features.astype(jnp.float32)
    inverse_rms = lax.rsqrt(jnp.mean(values * values, axis=-1, keepdims=True) + epsilon)
    return (values * inverse_rms).astype(jnp.bfloat16)


CH = 256


def filter_kernel(q_ref, r_ref, qt_ref, bias_ref, rt_ref, col_ref, row_ref, c_scr, h_scr):
    rows = q_ref.shape[0]
    lanes = r_ref.shape[0]
    chunks = lanes // CH
    hid = rt_ref.shape[0]
    cells = qt_ref.shape[1]
    depth = q_ref.shape[1]
    scale = math.sqrt(depth)
    qt = q_ref[...]
    for rc in range(chunks):
        corr = lax.dot_general(
            qt, r_ref[rc * CH:(rc + 1) * CH, :], (((1,), (1,)), ((), ())),
            preferred_element_type=jnp.float32,
        )
        c_scr[:, rc * CH:(rc + 1) * CH] = (corr / scale).astype(jnp.bfloat16)

    def per_query(p, carry):
        base = pl.multiple_of(p * cells, cells)
        for rc in range(chunks):
            cc = c_scr[pl.ds(base, cells), rc * CH:(rc + 1) * CH]
            for kg in range(hid // 4):
                hq = jnp.dot(
                    qt_ref[kg * 4 * cells:(kg + 1) * 4 * cells, :], cc,
                    preferred_element_type=jnp.float32,
                )
                hq = jnp.maximum(hq + bias_ref[kg * 4 * cells:(kg + 1) * 4 * cells, :], 0.0)
                hq = hq.astype(jnp.bfloat16)
                for kk in range(4):
                    k = kg * 4 + kk
                    h_scr[k, rc * cells:(rc + 1) * cells, :] = hq[kk * cells:(kk + 1) * cells, :]
        acc = jnp.dot(h_scr[0], rt_ref[0], preferred_element_type=jnp.float32)
        for k in range(1, hid):
            acc = acc + jnp.dot(h_scr[k], rt_ref[k], preferred_element_type=jnp.float32)
        col_ref[0, p] = jnp.max(acc.reshape(chunks, cells, CH), axis=1)
        accT = acc.T
        row_ref[0, p] = jnp.max(accT.reshape(CH // cells, cells, chunks * cells), axis=1)
        return carry

    lax.fori_loop(0, rows // cells, per_query, 0)


def local_scores(q_all, r_all, query_table, ref_table, tap_bias):
    nql, cells, depth = q_all.shape
    nrl = r_all.shape[0]
    hid = query_table.shape[0]
    qt_per = 4
    tiles = nql // qt_per
    chunks = nrl * cells // CH
    r4 = CH // cells
    qstack = query_table.reshape(hid * cells, cells)
    bias_col = jnp.repeat(tap_bias.astype(jnp.float32), cells)[:, None]
    eye = jnp.eye(r4, dtype=jnp.float32)
    rtT = jnp.transpose(ref_table.astype(jnp.float32), (0, 2, 1))
    rt = jnp.einsum("xy,kjb->kxjyb", eye, rtT).reshape(hid, CH, CH).astype(jnp.bfloat16)
    q2 = q_all.reshape(nql * cells, depth)
    r2 = r_all.reshape(nrl * cells, depth)
    col, row = pl.pallas_call(
        filter_kernel,
        grid=(tiles,),
        in_specs=[
            pl.BlockSpec((qt_per * cells, depth), lambda t: (t, 0)),
            pl.BlockSpec((nrl * cells, depth), lambda t: (0, 0)),
            pl.BlockSpec((hid * cells, cells), lambda t: (0, 0)),
            pl.BlockSpec((hid * cells, 1), lambda t: (0, 0)),
            pl.BlockSpec((hid, CH, CH), lambda t: (0, 0, 0)),
        ],
        out_specs=[
            pl.BlockSpec((1, qt_per, chunks, CH), lambda t: (t, 0, 0, 0)),
            pl.BlockSpec((1, qt_per, r4, chunks * cells), lambda t: (t, 0, 0, 0)),
        ],
        out_shape=[
            jax.ShapeDtypeStruct((tiles, qt_per, chunks, CH), jnp.float32),
            jax.ShapeDtypeStruct((tiles, qt_per, r4, chunks * cells), jnp.float32),
        ],
        scratch_shapes=[
            pltpu.VMEM((qt_per * cells, nrl * cells), jnp.bfloat16),
            pltpu.VMEM((hid, chunks * cells, CH), jnp.bfloat16),
        ],
        compiler_params=pltpu.CompilerParams(vmem_limit_bytes=48 * 1024 * 1024),
    )(q2, r2, qstack, bias_col, rt)
    col_pool = jnp.mean(col.reshape(tiles, qt_per, chunks, r4, cells), axis=-1)
    row_pool = jnp.mean(row.reshape(tiles, qt_per, r4, chunks, cells), axis=-1)
    row_pool = jnp.transpose(row_pool, (0, 1, 3, 2))
    return (0.5 * (row_pool + col_pool)).reshape(nql, nrl)


def shards(queries, references, query_taps, ref_taps, tap_bias, candidates):
    query_table = conv_table(query_taps, SIDE)
    ref_table = conv_table(ref_taps, SIDE)
    query_unit = normalize(queries)
    ref_unit = normalize(references)
    blk = lax.axis_size("blk")
    wide = lax.axis_size("wide")
    qt_per = query_unit.shape[0]
    rl = ref_unit.shape[0]
    q_all = lax.all_gather(query_unit, "blk", axis=0, tiled=True)
    r_all = lax.all_gather(ref_unit, "wide", axis=0, tiled=True)
    s = local_scores(q_all, r_all, query_table, ref_table, tap_bias)
    gathered = lax.all_gather(s, "blk", axis=0, tiled=False)
    me = lax.axis_index("blk")
    mine = lax.dynamic_slice_in_dim(gathered, me * qt_per, qt_per, axis=1)
    mine = mine.reshape(blk, qt_per, wide, rl)
    mine = jnp.transpose(mine, (1, 2, 0, 3)).reshape(qt_per, wide * blk * rl)
    block_refs = blk * rl
    keep = jnp.repeat(candidates[0] != 0, block_refs)
    return jnp.where(keep[None, :], mine, jnp.float32(0.0))


def solution(mesh):
    placed = (
        P(("wide", "blk"), None, None),
        P(("wide", "blk"), None, None),
        P(),
        P(),
        P(),
        P(("wide", "blk"), None),
    )
    return jax.shard_map(
        shards, mesh=mesh, in_specs=placed, out_specs=P(("wide", "blk"), None), check_vma=False
    )
```

time: 396 us -> 241 us (0.61)
  waiting for transfers between devices: 210 us -> 86.8 us
  Pallas kernels: 0 us -> 85.5 us
  matrix products: 80 us -> 0 us
  local copies, waits for them, and re-layouts: 69.7 us -> 13.2 us
  blocking collectives: 0 us -> 28.2 us
  loops' own time: 11.2 us -> 0 us
  other arithmetic: 9.25 us -> 13.4 us
    ppermute x15 -> x0, waiting for transfers between devices: 175 us -> none  [from_behind(): lax.ppermute(x, axis, [(i, (i + by) % length) for i in range(length)])]
    pallas_call x0 -> x1, Pallas kernels: none -> 85.5 us  [local_scores(): pl.pallas_call(filter_kernel, grid=(tiles,), in_specs=[pl.BlockSpec((qt_p...]
    dot_general x12 -> x0, matrix products: 80 us -> none  [the longest x6 69.8 us: pair_scores(): jnp.einsum('pkarj,kbj->parb', hidden, ref_table, preferred_element_type=j...]
    all_gather x1 -> x2, waiting for transfers between devices: 35.2 us -> 86.8 us  [the longest x1 50.8 us: shards(): r_all = lax.all_gather(ref_unit, 'wide', axis=0, tiled=True)]
    another operation x25 -> x3, local copies, waits for them, and re-layouts: 34.6 us -> 0.77 us  [the longest x1 0.47 us: local_scores(): bias_col = jnp.repeat(tap_bias.astype(jnp.float32), cells)[:, None]]
    all_gather x0 -> x1, blocking collectives: none -> 28.2 us  [shards(): gathered = lax.all_gather(s, 'blk', axis=0, tiled=False)]
    while x30 -> x0, local copies, waits for them, and re-layouts: 15.5 us -> none
    another operation x17 -> x0, loops' own time: 11.2 us -> none  [the longest x1 10.8 us: shards(): lax.fori_loop(0, cycle_size - 1, advance, (start_scores, carried))]
  transfers between devices with their start and end apart: 16 -> 2, of which waited for: 16 -> 2; matrix products, arithmetic and copies ran while one was open for 23% -> 7% of each run, Pallas kernels for 0% -> 0%
where the time goes in v1:
time: 241 us
  waiting for transfers between devices  86.8 us (36%)
  Pallas kernels  85.5 us (35%)
  blocking collectives  28.2 us (12%)
  between operations  13.5 us (6%)
  other arithmetic  13.4 us (6%)
  local copies, waits for them, and re-layouts  13.2 us (5%)
    pallas_call x1, Pallas kernels, local_scores(): pl.pallas_call(filter_kernel, grid=(tiles,), in_specs=[pl.BlockSpec((qt_p...  85.5 us
    all_gather x1, waiting for transfers between devices, shards(): r_all = lax.all_gather(ref_unit, 'wide', axis=0, tiled=True)  50.8 us
    all_gather x1, waiting for transfers between devices, shards(): q_all = lax.all_gather(query_unit, 'blk', axis=0, tiled=True)  35.9 us
    all_gather x1, blocking collectives, shards(): gathered = lax.all_gather(s, 'blk', axis=0, tiled=False)  28.2 us
    convert_element_type x1, local copies, waits for them, and re-layouts, local_scores(): jnp.einsum('xy,kjb->kxjyb', eye, rtT).reshape(hid, CH, CH)  6.98 us
  transfers between devices with their start and end apart: 2, of which 2 were waited for; matrix products, arithmetic and copies ran while one was open for 7% of the time, Pallas kernels for 0%

profile of v1, /device:TPU:0, one launch (start us, length us, event | category | flops | bytes accessed | tf_op | source)
XLA Modules:
  0.0 240.7 jit_solution(11538314529026408498)
XLA Ops:
  6.5 0.0 all-gather.3.cloned.1.call-start
  6.5 1.1 fusion.1
  7.6 1.8 fusion.2
  9.4 0.0 all-gather.3.cloned.1.call-update
  9.4 0.0 all-gather.5.cloned.1.call-start
  9.5 1.0 fusion.4
  10.5 1.6 fusion.5
  12.2 0.0 all-gather.5.cloned.1.call-update
  12.2 0.7 convert_element_type.43
  12.9 0.7 convert_element_type.46
  13.6 0.1 fusion.11
  13.7 0.1 fusion.8
  13.8 0.1 fusion.3
  13.8 1.4 select_reduce_fusion
  15.3 0.2 copy.29
  15.5 4.1 %fusion = bf16[16,4,64,4,64]{4,3,2,1,0:T(4,128)(2,1)} fusion(f32[4,4]{1,0:T(4,128)S(1)} %fusion.12, f32[16,64,64]{2,1,0:T(8,128)S(1)} %copy.29), kind=kLoop, calls=%fused_computation.3 | loop fusion | flops 2097152 | bytes 2359360 | tf_op jit(solution)/shard_map/convert_element_type | solution.py:95
  19.6 0.0 copy-start.2
  19.6 0.0 copy-start.3
  19.6 7.0 %convert_element_type.50.rt_ref = bf16[16,256,256]{2,1,0:T(8,128)(2,1)} reshape(bf16[16,4,64,4,64]{4,3,2,1,0:T(4,128)(2,1)} %fusion) | data formatting | bytes 4194304 | tf_op jit(solution)/shard_map/convert_element_type | solution.py:95
  26.6 0.0 copy-done.2
  26.6 0.1 broadcast_in_dim.77
  26.6 0.5 broadcast_in_dim_reshape.5.bias_ref
  27.1 0.0 copy-done.3
  27.1 0.1 broadcast_in_dim.71
  27.2 0.1 broadcast_in_dim.72
  27.3 35.9 %all-gather.3.cloned.1.call-done = bf16[32,64,512]{2,1,0:T(8,128)(2,1)} async-done(((bf16[4,64,512]{2,1,0:T(8,128)(2,1)}), bf16[32,64,512]{2,1,0:T(8,128)(2,1)}) %all-gather.3.cloned.1.call-update) | async-done | bytes 2097168 | tf_op jit(solution)/shard_map/all_gather | solution.py:137
  63.2 50.8 %all-gather.5.cloned.1.call-done = bf16[32,64,512]{2,1,0:T(8,128)(2,1)} async-done(((bf16[2,64,512]{2,1,0:T(8,128)(2,1)}), bf16[32,64,512]{2,1,0:T(8,128)(2,1)}) %all-gather.5.cloned.1.call-update) | async-done | bytes 2097168 | tf_op jit(solution)/shard_map/all_gather | solution.py:138
  114.1 0.0 copy-start
  114.1 1.6 copy-done
  115.7 0.0 copy-start.1
  115.7 1.6 copy-done.1
  117.2 85.5 %shard_map.64 = (f32[8,4,8,256]{3,2,1,0:T(8,128)S(1)}, f32[8,4,4,512]{3,2,1,0:T(4,128)S(1)}) custom-call(bf16[2048,512]{1,0:T(8,128)(2,1)S(1)} %bitcast.21, bf16[2048,512]{1,0:T(8,128)(2,1)S(1)} %bitcast.22, bf16[1024,64]{1,0:T(8,128)(2,1)S(1)} %bitcast.23, f32[1024,1]{1,0:T(8,128)S(1)} %broadcast_in_dim_reshape.5.bias_ref, ...), custom_call_target="tpu_custom_call" | custom-call | tf_op jit(solution)/shard_map/pallas_call | solution.py:98
  202.7 0.2 reshape.210
  203.0 0.3 reduce_sum.62
  203.3 0.3 copy.32
  203.6 0.2 reshape.209
  203.8 0.3 reduce_sum.60
  204.1 0.3 copy.33
  204.4 0.1 all_gather_reshape.3
  204.5 28.2 %all_gather.11 = f32[8,32,32]{2,1,0:T(8,128)S(1)} all-gather(f32[1,32,32]{2,1,0:T(8,128)S(1)} %all_gather_reshape.3), channel_id=1, replica_groups=mesh['wide'=16,'blk'=8] {'blk'}, dimensions={0}, use_global_device_ids=true | all-gather | bytes 36864 | tf_op jit(solution)/shard_map/all_gather | solution.py:140
  232.7 0.1 copy.34
  232.8 0.3 copy.35
  233.1 0.1 broadcast_select_fusion
  233.2 0.7 copy.36
  (8 shorter events, 0.1 us)
Async XLA Ops:
  6.5 56.7 %all-gather.3.cloned.1.call-start = ((), (), s32[]{:S(2)}) async-start(), calls=%async_computation | async-start | bytes 2359296 | tf_op jit(solution)/shard_map/all_gather | solution.py:137
  9.4 104.6 %all-gather.5.cloned.1.call-start = ((), (), s32[]{:S(2)}) async-start(), calls=%async_computation.1 | async-start | bytes 2228224 | tf_op jit(solution)/shard_map/all_gather | solution.py:138
  19.6 7.0 %copy-start.2 = (f32[16]{0:T(128)S(1)}, f32[16]{0:T(128)}, u32[]{:S(2)}) copy-start(f32[16]{0:T(128)} %param.10) | copy-start | bytes 196
  19.6 7.5 %copy-start.3 = (s32[1,16]{1,0:T(1,128)S(1)}, s32[1,16]{1,0:T(1,128)}, u32[]{:S(2)}) copy-start(s32[1,16]{1,0:T(1,128)} %param.11) | copy-start | bytes 196
  114.1 1.6 copy-start
  115.7 1.6 copy-start.1
Sparse Core Ops, SparseCore 0:
  9.6 53.6 all-gather.2
  65.7 48.3 all-gather.4

commit v2 on v1

--- a/solution.py
+++ b/solution.py
@@ -39,7 +39,7 @@
 CH = 256
 
 
-def filter_kernel(q_ref, r_ref, qt_ref, bias_ref, rt_ref, col_ref, row_ref, c_scr, h_scr):
+def filter_kernel(q_ref, r_ref, qt_ref, bias_ref, rtt_ref, col_ref, row_ref, c_scr, h_scr, rt_ref):
     rows = q_ref.shape[0]
     lanes = r_ref.shape[0]
     chunks = lanes // CH
@@ -47,6 +47,14 @@
     cells = qt_ref.shape[1]
     depth = q_ref.shape[1]
     scale = math.sqrt(depth)
+
+    @pl.when(pl.program_id(0) == 0)
+    def _():
+        rt_ref[...] = jnp.zeros(rt_ref.shape, rt_ref.dtype)
+        for k in range(hid):
+            blockk = rtt_ref[k]
+            for x in range(CH // cells):
+                rt_ref[k, x * cells:(x + 1) * cells, x * cells:(x + 1) * cells] = blockk
     qt = q_ref[...]
     for rc in range(chunks):
         corr = lax.dot_general(
@@ -90,9 +98,7 @@
     r4 = CH // cells
     qstack = query_table.reshape(hid * cells, cells)
     bias_col = jnp.repeat(tap_bias.astype(jnp.float32), cells)[:, None]
-    eye = jnp.eye(r4, dtype=jnp.float32)
-    rtT = jnp.transpose(ref_table.astype(jnp.float32), (0, 2, 1))
-    rt = jnp.einsum("xy,kjb->kxjyb", eye, rtT).reshape(hid, CH, CH).astype(jnp.bfloat16)
+    rtT = jnp.transpose(ref_table, (0, 2, 1))
     q2 = q_all.reshape(nql * cells, depth)
     r2 = r_all.reshape(nrl * cells, depth)
     col, row = pl.pallas_call(
@@ -103,7 +109,7 @@
             pl.BlockSpec((nrl * cells, depth), lambda t: (0, 0)),
             pl.BlockSpec((hid * cells, cells), lambda t: (0, 0)),
             pl.BlockSpec((hid * cells, 1), lambda t: (0, 0)),
-            pl.BlockSpec((hid, CH, CH), lambda t: (0, 0, 0)),
+            pl.BlockSpec((hid, cells, cells), lambda t: (0, 0, 0)),
         ],
         out_specs=[
             pl.BlockSpec((1, qt_per, chunks, CH), lambda t: (t, 0, 0, 0)),
@@ -116,9 +122,10 @@
         scratch_shapes=[
             pltpu.VMEM((qt_per * cells, nrl * cells), jnp.bfloat16),
             pltpu.VMEM((hid, chunks * cells, CH), jnp.bfloat16),
+            pltpu.VMEM((hid, CH, CH), jnp.bfloat16),
         ],
         compiler_params=pltpu.CompilerParams(vmem_limit_bytes=48 * 1024 * 1024),
-    )(q2, r2, qstack, bias_col, rt)
+    )(q2, r2, qstack, bias_col, rtT)
     col_pool = jnp.mean(col.reshape(tiles, qt_per, chunks, r4, cells), axis=-1)
     row_pool = jnp.mean(row.reshape(tiles, qt_per, r4, chunks, cells), axis=-1)
     row_pool = jnp.transpose(row_pool, (0, 1, 3, 2))
@@ -135,12 +142,19 @@
     qt_per = query_unit.shape[0]
     rl = ref_unit.shape[0]
     q_all = lax.all_gather(query_unit, "blk", axis=0, tiled=True)
-    r_all = lax.all_gather(ref_unit, "wide", axis=0, tiled=True)
-    s = local_scores(q_all, r_all, query_table, ref_table, tap_bias)
-    gathered = lax.all_gather(s, "blk", axis=0, tiled=False)
+    parts = []
+    for slot in range(rl):
+        r_slot = lax.all_gather(ref_unit[slot:slot + 1], "wide", axis=0, tiled=True)
+        parts.append(local_scores(q_all, r_slot, query_table, ref_table, tap_bias))
+    s = jnp.stack(parts, axis=-1).reshape(blk, qt_per, wide, rl)
     me = lax.axis_index("blk")
-    mine = lax.dynamic_slice_in_dim(gathered, me * qt_per, qt_per, axis=1)
-    mine = mine.reshape(blk, qt_per, wide, rl)
+    pieces = [lax.dynamic_index_in_dim(s, me, axis=0, keepdims=False)]
+    for d in range(1, blk):
+        send = lax.dynamic_index_in_dim(s, (me + d) % blk, axis=0, keepdims=False)
+        pieces.append(lax.ppermute(send, "blk", [(i, (i + d) % blk) for i in range(blk)]))
+    got = jnp.stack(pieces, axis=0)
+    order = (me - jnp.arange(blk)) % blk
+    mine = jnp.take(got, order, axis=0)
     mine = jnp.transpose(mine, (1, 2, 0, 3)).reshape(qt_per, wide * blk * rl)
     block_refs = blk * rl
     keep = jnp.repeat(candidates[0] != 0, block_refs)

time: 241 us -> 288 us (1.20)
  Pallas kernels: 85.5 us -> 146 us
  blocking collectives: 28.2 us -> 0 us
  starting transfers between devices: 0.04 us -> 10.6 us
  waiting for transfers between devices: 86.8 us -> 94.5 us
    pallas_call x1 -> x2, Pallas kernels: 85.5 us -> 146 us  [local_scores(): pl.pallas_call(filter_kernel, grid=(tiles,), in_specs=[pl.BlockSpec((qt_p...]
    all_gather x1 -> x0, blocking collectives: 28.2 us -> none  [shards(): gathered = lax.all_gather(s, 'blk', axis=0, tiled=False)]
    all_gather x1, waiting for transfers between devices: 35.9 us -> 52.4 us  [shards(): q_all = lax.all_gather(query_unit, 'blk', axis=0, tiled=True)]
    all_gather x1 -> x2, waiting for transfers between devices: 50.8 us -> 37.9 us  [shards(): r_slot = lax.all_gather(ref_unit[slot:slot + 1], 'wide', axis=0, tiled=True)]
    ppermute x0 -> x7, starting transfers between devices: none -> 10.5 us  [shards(): lax.ppermute(send, 'blk', [(i, (i + d) % blk) for i in range(blk)])]
    convert_element_type x1 -> x0, local copies, waits for them, and re-layouts: 6.98 us -> none  [local_scores(): jnp.einsum('xy,kjb->kxjyb', eye, rtT).reshape(hid, CH, CH)]
    convert_element_type x1 -> x0, other arithmetic: 4.07 us -> none  [local_scores(): jnp.einsum('xy,kjb->kxjyb', eye, rtT).reshape(hid, CH, CH)]
    ppermute x0 -> x7, waiting for transfers between devices: none -> 3.53 us  [shards(): lax.ppermute(send, 'blk', [(i, (i + d) % blk) for i in range(blk)])]
  transfers between devices with their start and end apart: 2 -> 10, of which waited for: 2 -> 4; matrix products, arithmetic and copies ran while one was open for 7% -> 5% of each run, Pallas kernels for 0% -> 25%
where the time goes in v2:
time: 288 us; the launch traced here: 287 us
  Pallas kernels  146 us (51%)
  waiting for transfers between devices  94.5 us (33%)
  between operations  13.4 us (5%)
  other arithmetic  12 us (4%)
  local copies, waits for them, and re-layouts  11.2 us (4%)
  starting transfers between devices  10.6 us (4%)
    pallas_call x2, Pallas kernels, local_scores(): pl.pallas_call(filter_kernel, grid=(tiles,), in_specs=[pl.BlockSpec((qt_p...  146 us
    all_gather x1, waiting for transfers between devices, shards(): q_all = lax.all_gather(query_unit, 'blk', axis=0, tiled=True)  52.4 us
    all_gather x2, waiting for transfers between devices, shards(): r_slot = lax.all_gather(ref_unit[slot:slot + 1], 'wide', axis=0, tiled=True)  37.9 us
    ppermute x7, starting transfers between devices, shards(): lax.ppermute(send, 'blk', [(i, (i + d) % blk) for i in range(blk)])  10.5 us
  transfers between devices with their start and end apart: 10, of which 4 were waited for; matrix products, arithmetic and copies ran while one was open for 5% of the time, Pallas kernels for 25%

profile of v2, /device:TPU:0, one launch (start us, length us, event | category | flops | bytes accessed | tf_op | source)
XLA Modules:
  0.0 287.5 jit_solution(5008229063647775227)
XLA Ops:
  6.5 1.0 fusion.3
  7.6 1.0 fusion.4
  8.6 0.7 fusion.30
  9.3 1.1 fusion
  10.4 1.8 fusion.1
  12.3 0.7 all-gather.6.cloned.1.call-update
  13.1 0.7 convert_element_type.39
  13.7 0.7 convert_element_type.36
  14.4 0.7 broadcast_in_dim.89
  15.2 0.5 broadcast_in_dim_reshape.6.bias_ref
  15.6 0.1 fusion.11
  15.9 1.4 select_reduce_fusion
  17.3 0.2 copy.45
  17.6 0.6 broadcast_in_dim.83
  18.2 0.5 compare_and_fusion
  18.7 0.6 pad_clamp_fusion
  19.3 37.9 %all-gather.8.cloned.1.call-done = bf16[16,64,512]{2,1,0:T(8,128)(2,1)} async-done(((bf16[1,64,512]{2,1,0:T(8,128)(2,1)}), bf16[16,64,512]{2,1,0:T(8,128)(2,1)}) %all-gather.8.cloned.1.call-update) | async-done | bytes 1048592 | tf_op jit(solution)/shard_map/all_gather | solution.py:147
  57.2 52.4 %all-gather.4.cloned.1.call-done = bf16[32,64,512]{2,1,0:T(8,128)(2,1)} async-done(((bf16[4,64,512]{2,1,0:T(8,128)(2,1)}), bf16[32,64,512]{2,1,0:T(8,128)(2,1)}) %all-gather.4.cloned.1.call-update) | async-done | bytes 2097168 | tf_op jit(solution)/shard_map/all_gather | solution.py:144
  109.5 1.6 copy-done
  111.1 1.2 copy-done.3
  112.3 72.9 %shard_map.65 = (f32[8,4,4,256]{3,2,1,0:T(4,128)S(1)}, f32[8,4,4,256]{3,2,1,0:T(4,128)S(1)}) custom-call(bf16[2048,512]{1,0:T(8,128)(2,1)S(1)} %bitcast.52, bf16[1024,512]{1,0:T(8,128)(2,1)S(1)} %bitcast.59, bf16[1024,64]{1,0:T(8,128)(2,1)S(1)} %bitcast.54, f32[1024,1]{1,0:T(8,128)S(1)} %broadcast_in_dim_reshape.6.bias_ref, bf16[16,64,64]{2,1,0:T(8,128)(2,1)S(1)} %bitcast.56), custom_call_target="tpu_custom_call" | custom-call | tf_op jit(solution)/shard_map/pallas_call | solution.py:104
  185.2 0.9 reshape.278
  186.1 1.2 reduce_sum.85
  187.3 0.8 copy.51
  188.1 0.2 reshape.277
  188.2 0.3 reduce_sum.83
  188.5 0.2 copy.50
  188.7 0.8 fusion.9
  189.5 1.2 copy-done.2
  190.8 72.9 %shard_map.64 = (f32[8,4,4,256]{3,2,1,0:T(4,128)S(1)}, f32[8,4,4,256]{3,2,1,0:T(4,128)S(1)}) custom-call(bf16[2048,512]{1,0:T(8,128)(2,1)S(1)} %bitcast.53, bf16[1024,512]{1,0:T(8,128)(2,1)S(1)} %bitcast.58, bf16[1024,64]{1,0:T(8,128)(2,1)S(1)} %bitcast.55, f32[1024,1]{1,0:T(8,128)S(1)} %broadcast_in_dim_reshape.6.bias_ref, bf16[16,64,64]{2,1,0:T(8,128)(2,1)S(1)} %bitcast.57), custom_call_target="tpu_custom_call" | custom-call | tf_op jit(solution)/shard_map/pallas_call | solution.py:104
  263.7 0.2 reshape.275
  263.8 0.3 reduce_sum.82
  264.1 0.2 copy.48
  264.3 0.2 reshape.274
  264.5 0.3 reduce_sum.80
  264.7 0.2 copy.47
  265.0 0.1 collective-permute-start
  265.1 1.7 collective-permute-start.1
  266.8 1.7 collective-permute-start.2
  268.6 2.3 collective-permute-start.3
  270.9 2.0 collective-permute-start.4
  272.9 2.6 collective-permute-start.5
  275.7 1.2 collective-permute-done.5
  276.9 2.3 collective-permute-done.6
  279.2 0.7 gather_fusion
  280.0 0.2 copy.54
  280.2 0.1 broadcast_select_fusion
  280.3 0.7 copy.55
  (44 shorter events, 0.7 us)
Async XLA Ops:
  6.5 10.9 %copy-start.6 = (s32[1,16]{1,0:T(1,128)S(1)}, s32[1,16]{1,0:T(1,128)}, u32[]{:S(2)}) copy-start(s32[1,16]{1,0:T(1,128)} %param.11) | copy-start | bytes 196
  6.5 50.6 %all-gather.8.cloned.1.call-start = ((), (), s32[]{:S(2)}) async-start(), calls=%async_computation.2 | async-start | bytes 1114112 | tf_op jit(solution)/shard_map/all_gather | solution.py:147
  9.3 100.2 %all-gather.4.cloned.1.call-start = ((), (), s32[]{:S(2)}) async-start(), calls=%async_computation | async-start | bytes 2359296 | tf_op jit(solution)/shard_map/all_gather | solution.py:144
  12.2 177.3 %all-gather.6.cloned.1.call-start = ((), (), s32[]{:S(2)}) async-start(), calls=%async_computation.1 | async-start | bytes 1114112 | tf_op jit(solution)/shard_map/all_gather | solution.py:147
  109.5 1.6 copy-start
  111.1 1.2 copy-start.3
  112.3 77.2 %copy-start.1 = (bf16[32,64,512]{2,1,0:T(8,128)(2,1)S(1)}, bf16[32,64,512]{2,1,0:T(8,128)(2,1)}, u32[]{:S(2)}) copy-start(bf16[32,64,512]{2,1,0:T(8,128)(2,1)} %all-gather.4.cloned.1.call-done) | copy-start | bytes 6291460
  189.5 1.2 copy-start.2
  263.7 16.2 %copy-start.5 = (pred[8]{0:T(512)(128)(4,1)S(1)}, pred[8]{0:T(512)(128)(4,1)}, u32[]{:S(2)}) copy-start(pred[8]{0:T(512)(128)(4,1)} %compare_and_fusion) | copy-start | bytes 28
  263.7 16.5 %copy-start.4 = (pred[256]{0:T(512)(128)(4,1)S(1)}, pred[256]{0:T(512)(128)(4,1)}, u32[]{:S(2)}) copy-start(pred[256]{0:T(512)(128)(4,1)} %broadcast_in_dim.83) | copy-start | bytes 772
  265.0 7.9 %collective-permute-start = (f32[4,16,2]{1,0,2:T(4,128)S(1)}, f32[4,16,2]{1,0,2:T(4,128)S(1)}, u32[]{:S(2)}, u32[]{:S(2)}) collective-permute-start(f32[4,16,2]{1,0,2:T(4,128)S(1)} %get-tuple-element.19), channel_id=1, source_target_pairs={{0,1},{1,2},{2,3},{3,4},{4,5},{5,6},{6,7},{7,0},{8,9},{9,10},{10,1... | collective-permute-start | bytes 1544 | tf_op jit(solution)/shard_map/ppermute | solution.py:154
  265.1 10.4 %collective-permute-start.1 = (f32[4,16,2]{1,0,2:T(4,128)S(1)}, f32[4,16,2]{1,0,2:T(4,128)S(1)}, u32[]{:S(2)}, u32[]{:S(2)}) collective-permute-start(f32[4,16,2]{1,0,2:T(4,128)S(1)} %get-tuple-element.20), channel_id=1, source_target_pairs={{0,2},{1,3},{2,4},{3,5},{4,6},{5,7},{6,0},{7,1},{8,10},{9,11},{10,... | collective-permute-start | bytes 1544 | tf_op jit(solution)/shard_map/ppermute | solution.py:154
  266.8 8.8 %collective-permute-start.2 = (f32[4,16,2]{1,0,2:T(4,128)S(1)}, f32[4,16,2]{1,0,2:T(4,128)S(1)}, u32[]{:S(2)}, u32[]{:S(2)}) collective-permute-start(f32[4,16,2]{1,0,2:T(4,128)S(1)} %get-tuple-element.21), channel_id=1, source_target_pairs={{0,3},{1,4},{2,5},{3,6},{4,7},{5,0},{6,1},{7,2},{8,11},{9,12},{10,... | collective-permute-start | bytes 1544 | tf_op jit(solution)/shard_map/ppermute | solution.py:154
  268.6 7.0 %collective-permute-start.3 = (f32[4,16,2]{1,0,2:T(4,128)S(1)}, f32[4,16,2]{1,0,2:T(4,128)S(1)}, u32[]{:S(2)}, u32[]{:S(2)}) collective-permute-start(f32[4,16,2]{1,0,2:T(4,128)S(1)} %get-tuple-element.22), channel_id=1, source_target_pairs={{0,4},{1,5},{2,6},{3,7},{4,0},{5,1},{6,2},{7,3},{8,12},{9,13},{10,... | collective-permute-start | bytes 1544 | tf_op jit(solution)/shard_map/ppermute | solution.py:154
  270.9 4.7 %collective-permute-start.4 = (f32[4,16,2]{1,0,2:T(4,128)S(1)}, f32[4,16,2]{1,0,2:T(4,128)S(1)}, u32[]{:S(2)}, u32[]{:S(2)}) collective-permute-start(f32[4,16,2]{1,0,2:T(4,128)S(1)} %get-tuple-element.24), channel_id=1, source_target_pairs={{0,5},{1,6},{2,7},{3,0},{4,1},{5,2},{6,3},{7,4},{8,13},{9,14},{10,... | collective-permute-start | bytes 1544 | tf_op jit(solution)/shard_map/ppermute | solution.py:154
  272.9 4.0 %collective-permute-start.5 = (f32[4,16,2]{1,0,2:T(4,128)S(1)}, f32[4,16,2]{1,0,2:T(4,128)S(1)}, u32[]{:S(2)}, u32[]{:S(2)}) collective-permute-start(f32[4,16,2]{1,0,2:T(4,128)S(1)} %get-tuple-element.23), channel_id=1, source_target_pairs={{0,6},{1,7},{2,0},{3,1},{4,2},{5,3},{6,4},{7,5},{8,14},{9,15},{10,... | collective-permute-start | bytes 1544 | tf_op jit(solution)/shard_map/ppermute | solution.py:154
  275.6 3.6 %collective-permute-start.6 = (f32[4,16,2]{1,0,2:T(4,128)S(1)}, f32[4,16,2]{1,0,2:T(4,128)S(1)}, u32[]{:S(2)}, u32[]{:S(2)}) collective-permute-start(f32[4,16,2]{1,0,2:T(4,128)S(1)} %get-tuple-element.17), channel_id=1, source_target_pairs={{0,7},{1,0},{2,1},{3,2},{4,3},{5,4},{6,5},{7,6},{8,15},{9,8},{10,9... | collective-permute-start | bytes 1544 | tf_op jit(solution)/shard_map/ppermute | solution.py:154
Sparse Core Ops, SparseCore 0:
  9.8 47.3 all-gather.7
  58.8 50.6 all-gather.3
  112.0 44.8 all-gather.5

commit v3 on v2

--- a/solution.py
+++ b/solution.py
@@ -39,7 +39,7 @@
 CH = 256
 
 
-def filter_kernel(q_ref, r_ref, qt_ref, bias_ref, rtt_ref, col_ref, row_ref, c_scr, h_scr, rt_ref):
+def filter_kernel(q_ref, r_ref, qt_ref, bias_ref, rtt_ref, col_ref, row_ref, c_scr, h_scr, rt_ref, f_scr):
     rows = q_ref.shape[0]
     lanes = r_ref.shape[0]
     chunks = lanes // CH
@@ -63,29 +63,30 @@
         )
         c_scr[:, rc * CH:(rc + 1) * CH] = (corr / scale).astype(jnp.bfloat16)
 
-    def per_query(p, carry):
-        base = pl.multiple_of(p * cells, cells)
+    nq = rows // cells
+    per = hid // 4
+    for p in range(nq):
         for rc in range(chunks):
-            cc = c_scr[pl.ds(base, cells), rc * CH:(rc + 1) * CH]
-            for kg in range(hid // 4):
+            cc = c_scr[p * cells:(p + 1) * cells, rc * CH:(rc + 1) * CH]
+            for kg in range(hid // per):
                 hq = jnp.dot(
-                    qt_ref[kg * 4 * cells:(kg + 1) * 4 * cells, :], cc,
+                    qt_ref[kg * per * cells:(kg + 1) * per * cells, :], cc,
                     preferred_element_type=jnp.float32,
                 )
-                hq = jnp.maximum(hq + bias_ref[kg * 4 * cells:(kg + 1) * 4 * cells, :], 0.0)
+                hq = jnp.maximum(hq + bias_ref[kg * per * cells:(kg + 1) * per * cells, :], 0.0)
                 hq = hq.astype(jnp.bfloat16)
-                for kk in range(4):
-                    k = kg * 4 + kk
-                    h_scr[k, rc * cells:(rc + 1) * cells, :] = hq[kk * cells:(kk + 1) * cells, :]
-        acc = jnp.dot(h_scr[0], rt_ref[0], preferred_element_type=jnp.float32)
-        for k in range(1, hid):
-            acc = acc + jnp.dot(h_scr[k], rt_ref[k], preferred_element_type=jnp.float32)
+                for kk in range(per):
+                    k = kg * per + kk
+                    row0 = (p * chunks + rc) * cells
+                    h_scr[k, row0:row0 + cells, :] = hq[kk * cells:(kk + 1) * cells, :]
+    f_scr[...] = jnp.dot(h_scr[0], rt_ref[0], preferred_element_type=jnp.float32)
+    for k in range(1, hid):
+        f_scr[...] += jnp.dot(h_scr[k], rt_ref[k], preferred_element_type=jnp.float32)
+    for p in range(nq):
+        acc = f_scr[p * chunks * cells:(p + 1) * chunks * cells, :]
         col_ref[0, p] = jnp.max(acc.reshape(chunks, cells, CH), axis=1)
         accT = acc.T
         row_ref[0, p] = jnp.max(accT.reshape(CH // cells, cells, chunks * cells), axis=1)
-        return carry
-
-    lax.fori_loop(0, rows // cells, per_query, 0)
 
 
 def local_scores(q_all, r_all, query_table, ref_table, tap_bias):
@@ -121,10 +122,11 @@
         ],
         scratch_shapes=[
             pltpu.VMEM((qt_per * cells, nrl * cells), jnp.bfloat16),
-            pltpu.VMEM((hid, chunks * cells, CH), jnp.bfloat16),
+            pltpu.VMEM((hid, qt_per * chunks * cells, CH), jnp.bfloat16),
             pltpu.VMEM((hid, CH, CH), jnp.bfloat16),
+            pltpu.VMEM((qt_per * chunks * cells, CH), jnp.float32),
         ],
-        compiler_params=pltpu.CompilerParams(vmem_limit_bytes=48 * 1024 * 1024),
+        compiler_params=pltpu.CompilerParams(vmem_limit_bytes=56 * 1024 * 1024),
     )(q2, r2, qstack, bias_col, rtT)
     col_pool = jnp.mean(col.reshape(tiles, qt_per, chunks, r4, cells), axis=-1)
     row_pool = jnp.mean(row.reshape(tiles, qt_per, r4, chunks, cells), axis=-1)
@@ -141,19 +143,23 @@
     wide = lax.axis_size("wide")
     qt_per = query_unit.shape[0]
     rl = ref_unit.shape[0]
-    q_all = lax.all_gather(query_unit, "blk", axis=0, tiled=True)
+    shifts = [query_unit] + [
+        lax.ppermute(query_unit, "blk", [(i, (i + d) % blk) for i in range(blk)])
+        for d in range(1, blk)
+    ]
+    q_all = jnp.concatenate(shifts, axis=0)
     parts = []
     for slot in range(rl):
         r_slot = lax.all_gather(ref_unit[slot:slot + 1], "wide", axis=0, tiled=True)
         parts.append(local_scores(q_all, r_slot, query_table, ref_table, tap_bias))
     s = jnp.stack(parts, axis=-1).reshape(blk, qt_per, wide, rl)
     me = lax.axis_index("blk")
-    pieces = [lax.dynamic_index_in_dim(s, me, axis=0, keepdims=False)]
-    for d in range(1, blk):
-        send = lax.dynamic_index_in_dim(s, (me + d) % blk, axis=0, keepdims=False)
-        pieces.append(lax.ppermute(send, "blk", [(i, (i + d) % blk) for i in range(blk)]))
+    pieces = [s[0]] + [
+        lax.ppermute(s[d], "blk", [(i, (i - d) % blk) for i in range(blk)])
+        for d in range(1, blk)
+    ]
     got = jnp.stack(pieces, axis=0)
-    order = (me - jnp.arange(blk)) % blk
+    order = (jnp.arange(blk) - me) % blk
     mine = jnp.take(got, order, axis=0)
     mine = jnp.transpose(mine, (1, 2, 0, 3)).reshape(qt_per, wide * blk * rl)
     block_refs = blk * rl

time: 288 us -> 181 us (0.63)
  Pallas kernels: 146 us -> 84.3 us
  waiting for transfers between devices: 94.5 us -> 36.6 us
  starting transfers between devices: 10.6 us -> 23.1 us
    pallas_call x2, Pallas kernels: 146 us -> 84.3 us  [local_scores(): pl.pallas_call(filter_kernel, grid=(tiles,), in_specs=[pl.BlockSpec((qt_p...]
    all_gather x1 -> x0, waiting for transfers between devices: 52.4 us -> none  [shards(): q_all = lax.all_gather(query_unit, 'blk', axis=0, tiled=True)]
    all_gather x2, waiting for transfers between devices: 37.9 us -> 20.5 us  [shards(): r_slot = lax.all_gather(ref_unit[slot:slot + 1], 'wide', axis=0, tiled=True)]
    ppermute x7 -> x14, waiting for transfers between devices: 3.53 us -> 16.1 us  [the longest x7 13.1 us: shards(): lax.ppermute(query_unit, 'blk', [(i, (i + d) % blk) for i in range(blk)])]
    ppermute x7 -> x14, starting transfers between devices: 10.5 us -> 23 us  [the longest x7 12.2 us: shards(): lax.ppermute(query_unit, 'blk', [(i, (i + d) % blk) for i in range(blk)])]
  transfers between devices with their start and end apart: 10 -> 16, of which waited for: 4 -> 7; matrix products, arithmetic and copies ran while one was open for 5% -> 8% of each run, Pallas kernels for 25% -> 23%
where the time goes in v3:
time: 181 us; the launch traced here: 180 us
  Pallas kernels  84.3 us (47%)
  waiting for transfers between devices  36.6 us (20%)
  starting transfers between devices  23.1 us (13%)
  between operations  13.6 us (8%)
  local copies, waits for them, and re-layouts  12.9 us (7%)
  other arithmetic  9.76 us (5%)
    pallas_call x2, Pallas kernels, local_scores(): pl.pallas_call(filter_kernel, grid=(tiles,), in_specs=[pl.BlockSpec((qt_p...  84.3 us
    all_gather x2, waiting for transfers between devices, shards(): r_slot = lax.all_gather(ref_unit[slot:slot + 1], 'wide', axis=0, tiled=True)  20.5 us
    ppermute x7, waiting for transfers between devices, shards(): lax.ppermute(query_unit, 'blk', [(i, (i + d) % blk) for i in range(blk)])  13.1 us
    ppermute x7, starting transfers between devices, shards(): lax.ppermute(query_unit, 'blk', [(i, (i + d) % blk) for i in range(blk)])  12.2 us
    ppermute x7, starting transfers between devices, shards(): lax.ppermute(s[d], 'blk', [(i, (i - d) % blk) for i in range(blk)])  10.8 us
  transfers between devices with their start and end apart: 16, of which 7 were waited for; matrix products, arithmetic and copies ran while one was open for 8% of the time, Pallas kernels for 23%

profile of v3, /device:TPU:0, one launch (start us, length us, event | category | flops | bytes accessed | tf_op | source)
XLA Modules:
  0.0 180.2 jit_solution(8743924295057048119)
XLA Ops:
  6.5 1.0 fusion.3
  7.6 1.0 fusion.4
  8.6 0.7 fusion.16
  9.3 1.1 fusion
  10.4 1.1 constant_dynamic-update-slice_fusion.7
  11.5 1.8 collective-permute-start
  13.2 1.5 collective-permute-start.1
  14.7 2.0 %collective-permute-start.2 = (bf16[4,64,512]{2,1,0:T(8,128)(2,1)S(1)}, bf16[4,64,512]{2,1,0:T(8,128)(2,1)S(1)}, u32[]{:S(2)}, u32[]{:S(2)}) collective-permute-start(bf16[4,64,512]{2,1,0:T(8,128)(2,1)S(1)} %get-tuple-element.16), channel_id=1, source_target_pairs={{0,3},{1,4},{2,5},{3,6},{4,7},{5,0},{6,1},{7,2},{8,11},{9,12},{10,... | collective-permute-start | bytes 786440 | tf_op jit(solution)/shard_map/ppermute | solution.py:147
  16.7 2.0 %collective-permute-start.3 = (bf16[4,64,512]{2,1,0:T(8,128)(2,1)S(1)}, bf16[4,64,512]{2,1,0:T(8,128)(2,1)S(1)}, u32[]{:S(2)}, u32[]{:S(2)}) collective-permute-start(bf16[4,64,512]{2,1,0:T(8,128)(2,1)S(1)} %get-tuple-element.16), channel_id=1, source_target_pairs={{0,4},{1,5},{2,6},{3,7},{4,0},{5,1},{6,2},{7,3},{8,12},{9,13},{10,... | collective-permute-start | bytes 786440 | tf_op jit(solution)/shard_map/ppermute | solution.py:147
  18.7 3.1 %collective-permute-start.4 = (bf16[4,64,512]{2,1,0:T(8,128)(2,1)S(1)}, bf16[4,64,512]{2,1,0:T(8,128)(2,1)S(1)}, u32[]{:S(2)}, u32[]{:S(2)}) collective-permute-start(bf16[4,64,512]{2,1,0:T(8,128)(2,1)S(1)} %get-tuple-element.16), channel_id=1, source_target_pairs={{0,5},{1,6},{2,7},{3,0},{4,1},{5,2},{6,3},{7,4},{8,13},{9,14},{10,... | collective-permute-start | bytes 786440 | tf_op jit(solution)/shard_map/ppermute | solution.py:147
  22.1 0.7 compare_bitcast_fusion
  22.8 0.7 convert_element_type.36
  23.4 0.7 convert_element_type.39
  24.2 2.0 %select_reduce_fusion = (bf16[16,64,64]{2,1,0:T(8,128)(2,1)S(1)}, bf16[16,64,64]{2,1,0:T(8,128)(2,1)}) fusion(f32[16,9]{1,0:T(8,128)S(1)} %convert_element_type.39, pred[9,64,64]{2,1,0:T(8,128)(4,1)S(1)} %fusion.2, f32[16,9]{1,0:T(8,128)S(1)} %convert_element_type.36), kind=kLoop, calls=%fused_computation.1 | loop fusion | flops 2228224 | bytes 300160 | tf_op jit(solution)/shard_map/reduce_sum | solution.py:26
  26.3 0.9 copy.52
  27.2 1.3 broadcast_in_dim_reshape.6.bias_ref
  28.7 1.5 collective-permute-start.5
  30.2 1.0 constant_dynamic-update-slice_fusion.6
  31.1 0.3 collective-permute-start.6
  31.4 1.0 constant_dynamic-update-slice_fusion.5
  32.4 5.6 %collective-permute-done.2 = bf16[4,64,512]{2,1,0:T(8,128)(2,1)S(1)} collective-permute-done((bf16[4,64,512]{2,1,0:T(8,128)(2,1)S(1)}, bf16[4,64,512]{2,1,0:T(8,128)(2,1)S(1)}, u32[]{:S(2)}, u32[]{:S(2)}) %collective-permute-start.2) | collective-permute-done | bytes 262176 | tf_op jit(solution)/shard_map/ppermute | solution.py:147
  38.1 3.0 %collective-permute-done.4 = bf16[4,64,512]{2,1,0:T(8,128)(2,1)S(1)} collective-permute-done((bf16[4,64,512]{2,1,0:T(8,128)(2,1)S(1)}, bf16[4,64,512]{2,1,0:T(8,128)(2,1)S(1)}, u32[]{:S(2)}, u32[]{:S(2)}) %collective-permute-start.4) | collective-permute-done | bytes 262176 | tf_op jit(solution)/shard_map/ppermute | solution.py:147
  41.1 4.4 %collective-permute-done.6 = bf16[4,64,512]{2,1,0:T(8,128)(2,1)S(1)} collective-permute-done((bf16[4,64,512]{2,1,0:T(8,128)(2,1)S(1)}, bf16[4,64,512]{2,1,0:T(8,128)(2,1)S(1)}, u32[]{:S(2)}, u32[]{:S(2)}) %collective-permute-start.6) | collective-permute-done | bytes 262176 | tf_op jit(solution)/shard_map/ppermute | solution.py:147
  45.6 19.7 %all-gather.5.cloned.1.call-done = bf16[16,64,512]{2,1,0:T(8,128)(2,1)} async-done(((bf16[1,64,512]{2,1,0:T(8,128)(2,1)}), bf16[16,64,512]{2,1,0:T(8,128)(2,1)}) %all-gather.5.cloned.1.call-update) | async-done | bytes 1048592 | tf_op jit(solution)/shard_map/all_gather | solution.py:153
  65.3 42.1 %shard_map.65 = (f32[8,4,4,256]{3,2,1,0:T(4,128)}, f32[8,4,4,256]{3,2,1,0:T(4,128)}) custom-call(bf16[2048,512]{1,0:T(8,128)(2,1)} %bitcast.46, bf16[1024,512]{1,0:T(8,128)(2,1)} %bitcast.52, bf16[1024,64]{1,0:T(8,128)(2,1)} %bitcast.48, f32[1024,1]{1,0:T(8,128)} %broadcast_in_dim_reshape.6.bias_ref, bf16[16,64,64]{2,1,0:T(8,128)(2,1)} %bitcast.50), custom_call_target="tpu_custom_call" | custom-call | tf_op jit(solution)/shard_map/pallas_call | solution.py:105
  107.4 1.1 reshape.288
  108.4 0.3 reduce_sum.83
  108.9 1.1 reshape.289
  110.0 0.3 reduce_sum.85
  110.2 0.2 copy.59
  110.7 0.8 all-gather.3.cloned.1.call-done
  111.4 42.2 %shard_map.64 = (f32[8,4,4,256]{3,2,1,0:T(4,128)}, f32[8,4,4,256]{3,2,1,0:T(4,128)}) custom-call(bf16[2048,512]{1,0:T(8,128)(2,1)} %bitcast.47, bf16[1024,512]{1,0:T(8,128)(2,1)} %bitcast.53, bf16[1024,64]{1,0:T(8,128)(2,1)} %bitcast.49, f32[1024,1]{1,0:T(8,128)} %broadcast_in_dim_reshape.6.bias_ref, bf16[16,64,64]{2,1,0:T(8,128)(2,1)} %bitcast.51), custom_call_target="tpu_custom_call" | custom-call | tf_op jit(solution)/shard_map/pallas_call | solution.py:105
  153.6 1.1 reshape.285
  154.7 0.3 reduce_sum.80
  155.1 1.1 reshape.286
  156.2 0.3 reduce_sum.82
  156.5 0.2 copy.55
  157.1 2.7 %collective-permute-start.7 = (f32[4,16,2]{0,1,2:T(8,128)S(1)}, f32[4,16,2]{0,1,2:T(8,128)S(1)}, u32[]{:S(2)}, u32[]{:S(2)}) collective-permute-start(f32[4,16,2]{0,1,2:T(8,128)S(1)} %get-tuple-element.25), channel_id=1, source_target_pairs={{0,7},{1,0},{2,1},{3,2},{4,3},{5,4},{6,5},{7,6},{8,15},{9,8},{10,9... | collective-permute-start | bytes 1544 | tf_op jit(solution)/shard_map/ppermute | solution.py:158
  159.8 0.9 collective-permute-start.8
  160.7 1.4 collective-permute-start.9
  162.1 2.7 %collective-permute-start.10 = (f32[4,16,2]{0,1,2:T(8,128)S(1)}, f32[4,16,2]{0,1,2:T(8,128)S(1)}, u32[]{:S(2)}, u32[]{:S(2)}) collective-permute-start(f32[4,16,2]{0,1,2:T(8,128)S(1)} %get-tuple-element.22), channel_id=1, source_target_pairs={{0,4},{1,5},{2,6},{3,7},{4,0},{5,1},{6,2},{7,3},{8,12},{9,13},{10,... | collective-permute-start | bytes 1544 | tf_op jit(solution)/shard_map/ppermute | solution.py:158
  164.8 0.8 collective-permute-start.12
  165.6 2.4 %collective-permute-start.13 = (f32[4,16,2]{0,1,2:T(8,128)S(1)}, f32[4,16,2]{0,1,2:T(8,128)S(1)}, u32[]{:S(2)}, u32[]{:S(2)}) collective-permute-start(f32[4,16,2]{0,1,2:T(8,128)S(1)} %get-tuple-element.19), channel_id=1, source_target_pairs={{0,1},{1,2},{2,3},{3,4},{4,5},{5,6},{6,7},{7,0},{8,9},{9,10},{10,1... | collective-permute-start | bytes 1544 | tf_op jit(solution)/shard_map/ppermute | solution.py:158
  168.4 2.5 %collective-permute-done.11 = f32[4,16,2]{0,1,2:T(8,128)S(1)} collective-permute-done((f32[4,16,2]{0,1,2:T(8,128)S(1)}, f32[4,16,2]{0,1,2:T(8,128)S(1)}, u32[]{:S(2)}, u32[]{:S(2)}) %collective-permute-start.11) | collective-permute-done | bytes 544 | tf_op jit(solution)/shard_map/ppermute | solution.py:158
  171.1 0.5 collective-permute-done.13
  171.7 0.6 gather_fusion
  172.4 0.2 copy.69
  172.7 0.7 copy.70
  (64 shorter events, 2.6 us)
Async XLA Ops:
  6.5 20.6 %copy-start.1 = (f32[16]{0:T(128)S(1)}, f32[16]{0:T(128)}, u32[]{:S(2)}) copy-start(f32[16]{0:T(128)} %param.10) | copy-start | bytes 196
  6.5 58.7 %all-gather.5.cloned.1.call-start = ((), (), s32[]{:S(2)}) async-start(), calls=%async_computation.1 | async-start | bytes 1114112 | tf_op jit(solution)/shard_map/all_gather | solution.py:153
  9.3 102.2 %all-gather.3.cloned.1.call-start = ((), (), s32[]{:S(2)}) async-start(), calls=%async_computation | async-start | bytes 1114112 | tf_op jit(solution)/shard_map/all_gather | solution.py:153
  11.5 17.2 %collective-permute-start = (bf16[4,64,512]{2,1,0:T(8,128)(2,1)S(1)}, bf16[4,64,512]{2,1,0:T(8,128)(2,1)}, u32[]{:S(2)}, u32[]{:S(2)}) collective-permute-start(bf16[4,64,512]{2,1,0:T(8,128)(2,1)S(1)} %get-tuple-element.16), channel_id=1, source_target_pairs={{0,1},{1,2},{2,3},{3,4},{4,5},{5,6},{6,7},{7,0},{8,9},{9,10},{10,1... | collective-permute-start | bytes 786440 | tf_op jit(solution)/shard_map/ppermute | solution.py:147
  13.2 17.9 %collective-permute-start.1 = (bf16[4,64,512]{2,1,0:T(8,128)(2,1)S(1)}, bf16[4,64,512]{2,1,0:T(8,128)(2,1)}, u32[]{:S(2)}, u32[]{:S(2)}) collective-permute-start(bf16[4,64,512]{2,1,0:T(8,128)(2,1)S(1)} %get-tuple-element.16), channel_id=1, source_target_pairs={{0,2},{1,3},{2,4},{3,5},{4,6},{5,7},{6,0},{7,1},{8,10},{9,11},{10,... | collective-permute-start | bytes 786440 | tf_op jit(solution)/shard_map/ppermute | solution.py:147
  14.7 23.3 %collective-permute-start.2 = (bf16[4,64,512]{2,1,0:T(8,128)(2,1)S(1)}, bf16[4,64,512]{2,1,0:T(8,128)(2,1)S(1)}, u32[]{:S(2)}, u32[]{:S(2)}) collective-permute-start(bf16[4,64,512]{2,1,0:T(8,128)(2,1)S(1)} %get-tuple-element.16), channel_id=1, source_target_pairs={{0,3},{1,4},{2,5},{3,6},{4,7},{5,0},{6,1},{7,2},{8,11},{9,12},{10,... | collective-permute-start | bytes 786440 | tf_op jit(solution)/shard_map/ppermute | solution.py:147
  16.7 21.3 %collective-permute-start.3 = (bf16[4,64,512]{2,1,0:T(8,128)(2,1)S(1)}, bf16[4,64,512]{2,1,0:T(8,128)(2,1)S(1)}, u32[]{:S(2)}, u32[]{:S(2)}) collective-permute-start(bf16[4,64,512]{2,1,0:T(8,128)(2,1)S(1)} %get-tuple-element.16), channel_id=1, source_target_pairs={{0,4},{1,5},{2,6},{3,7},{4,0},{5,1},{6,2},{7,3},{8,12},{9,13},{10,... | collective-permute-start | bytes 786440 | tf_op jit(solution)/shard_map/ppermute | solution.py:147
  18.7 22.3 %collective-permute-start.4 = (bf16[4,64,512]{2,1,0:T(8,128)(2,1)S(1)}, bf16[4,64,512]{2,1,0:T(8,128)(2,1)S(1)}, u32[]{:S(2)}, u32[]{:S(2)}) collective-permute-start(bf16[4,64,512]{2,1,0:T(8,128)(2,1)S(1)} %get-tuple-element.16), channel_id=1, source_target_pairs={{0,5},{1,6},{2,7},{3,0},{4,1},{5,2},{6,3},{7,4},{8,13},{9,14},{10,... | collective-permute-start | bytes 786440 | tf_op jit(solution)/shard_map/ppermute | solution.py:147
  28.7 12.4 %collective-permute-start.5 = (bf16[4,64,512]{2,1,0:T(8,128)(2,1)S(1)}, bf16[4,64,512]{2,1,0:T(8,128)(2,1)S(1)}, u32[]{:S(2)}, u32[]{:S(2)}) collective-permute-start(bf16[4,64,512]{2,1,0:T(8,128)(2,1)S(1)} %get-tuple-element.16), channel_id=1, source_target_pairs={{0,6},{1,7},{2,0},{3,1},{4,2},{5,3},{6,4},{7,5},{8,14},{9,15},{10,... | collective-permute-start | bytes 786440 | tf_op jit(solution)/shard_map/ppermute | solution.py:147
  31.1 14.4 %collective-permute-start.6 = (bf16[4,64,512]{2,1,0:T(8,128)(2,1)S(1)}, bf16[4,64,512]{2,1,0:T(8,128)(2,1)S(1)}, u32[]{:S(2)}, u32[]{:S(2)}) collective-permute-start(bf16[4,64,512]{2,1,0:T(8,128)(2,1)S(1)} %get-tuple-element.16), channel_id=1, source_target_pairs={{0,7},{1,0},{2,1},{3,2},{4,3},{5,4},{6,5},{7,6},{8,15},{9,8},{10,9... | collective-permute-start | bytes 786440 | tf_op jit(solution)/shard_map/ppermute | solution.py:147
  45.6 19.7 %copy-start = (bf16[32,64,512]{2,1,0:T(8,128)(2,1)}, bf16[32,64,512]{2,1,0:T(8,128)(2,1)S(1)}, u32[]{:S(2)}) copy-start(bf16[32,64,512]{2,1,0:T(8,128)(2,1)S(1)} %constant_dynamic-update-slice_fusion) | copy-start | bytes 6291460
  157.1 7.6 %collective-permute-start.7 = (f32[4,16,2]{0,1,2:T(8,128)S(1)}, f32[4,16,2]{0,1,2:T(8,128)S(1)}, u32[]{:S(2)}, u32[]{:S(2)}) collective-permute-start(f32[4,16,2]{0,1,2:T(8,128)S(1)} %get-tuple-element.25), channel_id=1, source_target_pairs={{0,7},{1,0},{2,1},{3,2},{4,3},{5,4},{6,5},{7,6},{8,15},{9,8},{10,9... | collective-permute-start | bytes 1544 | tf_op jit(solution)/shard_map/ppermute | solution.py:158
  159.8 5.9 %collective-permute-start.8 = (f32[4,16,2]{0,1,2:T(8,128)S(1)}, f32[4,16,2]{0,1,2:T(8,128)S(1)}, u32[]{:S(2)}, u32[]{:S(2)}) collective-permute-start(f32[4,16,2]{0,1,2:T(8,128)S(1)} %get-tuple-element.24), channel_id=1, source_target_pairs={{0,6},{1,7},{2,0},{3,1},{4,2},{5,3},{6,4},{7,5},{8,14},{9,15},{10,... | collective-permute-start | bytes 1544 | tf_op jit(solution)/shard_map/ppermute | solution.py:158
  160.7 7.5 %collective-permute-start.9 = (f32[4,16,2]{0,1,2:T(8,128)S(1)}, f32[4,16,2]{0,1,2:T(8,128)S(1)}, u32[]{:S(2)}, u32[]{:S(2)}) collective-permute-start(f32[4,16,2]{0,1,2:T(8,128)S(1)} %get-tuple-element.23), channel_id=1, source_target_pairs={{0,5},{1,6},{2,7},{3,0},{4,1},{5,2},{6,3},{7,4},{8,13},{9,14},{10,... | collective-permute-start | bytes 1544 | tf_op jit(solution)/shard_map/ppermute | solution.py:158
  162.1 6.2 %collective-permute-start.10 = (f32[4,16,2]{0,1,2:T(8,128)S(1)}, f32[4,16,2]{0,1,2:T(8,128)S(1)}, u32[]{:S(2)}, u32[]{:S(2)}) collective-permute-start(f32[4,16,2]{0,1,2:T(8,128)S(1)} %get-tuple-element.22), channel_id=1, source_target_pairs={{0,4},{1,5},{2,6},{3,7},{4,0},{5,1},{6,2},{7,3},{8,12},{9,13},{10,... | collective-permute-start | bytes 1544 | tf_op jit(solution)/shard_map/ppermute | solution.py:158
  164.8 6.1 %collective-permute-start.11 = (f32[4,16,2]{0,1,2:T(8,128)S(1)}, f32[4,16,2]{0,1,2:T(8,128)S(1)}, u32[]{:S(2)}, u32[]{:S(2)}) collective-permute-start(f32[4,16,2]{0,1,2:T(8,128)S(1)} %get-tuple-element.21), channel_id=1, source_target_pairs={{0,3},{1,4},{2,5},{3,6},{4,7},{5,0},{6,1},{7,2},{8,11},{9,12},{10,... | collective-permute-start | bytes 1544 | tf_op jit(solution)/shard_map/ppermute | solution.py:158
  164.8 6.2 %collective-permute-start.12 = (f32[4,16,2]{0,1,2:T(8,128)S(1)}, f32[4,16,2]{0,1,2:T(8,128)S(1)}, u32[]{:S(2)}, u32[]{:S(2)}) collective-permute-start(f32[4,16,2]{0,1,2:T(8,128)S(1)} %get-tuple-element.20), channel_id=1, source_target_pairs={{0,2},{1,3},{2,4},{3,5},{4,6},{5,7},{6,0},{7,1},{8,10},{9,11},{10,... | collective-permute-start | bytes 1544 | tf_op jit(solution)/shard_map/ppermute | solution.py:158
  165.6 6.0 %collective-permute-start.13 = (f32[4,16,2]{0,1,2:T(8,128)S(1)}, f32[4,16,2]{0,1,2:T(8,128)S(1)}, u32[]{:S(2)}, u32[]{:S(2)}) collective-permute-start(f32[4,16,2]{0,1,2:T(8,128)S(1)} %get-tuple-element.19), channel_id=1, source_target_pairs={{0,1},{1,2},{2,3},{3,4},{4,5},{5,6},{6,7},{7,0},{8,9},{9,10},{10,1... | collective-permute-start | bytes 1544 | tf_op jit(solution)/shard_map/ppermute | solution.py:158
Sparse Core Ops, SparseCore 0:
  9.8 55.4 all-gather.4
  67.7 43.6 all-gather.2

commit v4 on v3

--- a/solution.py
+++ b/solution.py
@@ -154,13 +154,8 @@
         parts.append(local_scores(q_all, r_slot, query_table, ref_table, tap_bias))
     s = jnp.stack(parts, axis=-1).reshape(blk, qt_per, wide, rl)
     me = lax.axis_index("blk")
-    pieces = [s[0]] + [
-        lax.ppermute(s[d], "blk", [(i, (i - d) % blk) for i in range(blk)])
-        for d in range(1, blk)
-    ]
-    got = jnp.stack(pieces, axis=0)
-    order = (jnp.arange(blk) - me) % blk
-    mine = jnp.take(got, order, axis=0)
+    outgoing = jnp.take(s, (me - jnp.arange(blk)) % blk, axis=0)
+    mine = lax.all_to_all(outgoing, "blk", 0, 0, tiled=True)
     mine = jnp.transpose(mine, (1, 2, 0, 3)).reshape(qt_per, wide * blk * rl)
     block_refs = blk * rl
     keep = jnp.repeat(candidates[0] != 0, block_refs)

time: 181 us -> 178 us (0.983)
  starting transfers between devices: 23.1 us -> 17.2 us
  waiting for transfers between devices: 36.6 us -> 39.7 us
    ppermute x7 -> x0, starting transfers between devices: 10.8 us -> none  [shards(): lax.ppermute(s[d], 'blk', [(i, (i - d) % blk) for i in range(blk)])]
    all_to_all x0 -> x1, waiting for transfers between devices: none -> 5.92 us  [shards(): mine = lax.all_to_all(outgoing, 'blk', 0, 0, tiled=True)]
    all_to_all x0 -> x1, starting transfers between devices: none -> 4.25 us  [shards(): mine = lax.all_to_all(outgoing, 'blk', 0, 0, tiled=True)]
    ppermute x7 -> x0, waiting for transfers between devices: 3.08 us -> none  [shards(): lax.ppermute(s[d], 'blk', [(i, (i - d) % blk) for i in range(blk)])]
  transfers between devices with their start and end apart: 16 -> 10, of which waited for: 7 -> 6; matrix products, arithmetic and copies ran while one was open for 8% -> 8% of each run, Pallas kernels for 23% -> 24%
where the time goes in v4:
time: 178 us
  Pallas kernels  84.3 us (47%)
  waiting for transfers between devices  39.7 us (22%)
  starting transfers between devices  17.2 us (10%)
  between operations  13.6 us (8%)
  local copies, waits for them, and re-layouts  13 us (7%)
  other arithmetic  9.77 us (5%)
    pallas_call x2, Pallas kernels, local_scores(): pl.pallas_call(filter_kernel, grid=(tiles,), in_specs=[pl.BlockSpec((qt_p...  84.3 us
    all_gather x2, waiting for transfers between devices, shards(): r_slot = lax.all_gather(ref_unit[slot:slot + 1], 'wide', axis=0, tiled=True)  20.5 us
    ppermute x7, waiting for transfers between devices, shards(): lax.ppermute(query_unit, 'blk', [(i, (i + d) % blk) for i in range(blk)])  13.2 us
    ppermute x7, starting transfers between devices, shards(): lax.ppermute(query_unit, 'blk', [(i, (i + d) % blk) for i in range(blk)])  12.9 us
    all_to_all x1, waiting for transfers between devices, shards(): mine = lax.all_to_all(outgoing, 'blk', 0, 0, tiled=True)  5.92 us
    all_to_all x1, starting transfers between devices, shards(): mine = lax.all_to_all(outgoing, 'blk', 0, 0, tiled=True)  4.25 us
  transfers between devices with their start and end apart: 10, of which 6 were waited for; matrix products, arithmetic and copies ran while one was open for 8% of the time, Pallas kernels for 24%

profile of v4, /device:TPU:0, one launch (start us, length us, event | category | flops | bytes accessed | tf_op | source)
XLA Modules:
  0.0 177.5 jit_solution(6136289216808052194)
XLA Ops:
  6.5 1.0 fusion.3
  7.6 1.0 fusion.4
  8.6 0.7 fusion.16
  9.3 1.1 fusion
  10.4 1.1 constant_dynamic-update-slice_fusion.7
  11.5 1.8 collective-permute-start
  13.2 1.5 collective-permute-start.1
  14.7 2.0 %collective-permute-start.2 = (bf16[4,64,512]{2,1,0:T(8,128)(2,1)S(1)}, bf16[4,64,512]{2,1,0:T(8,128)(2,1)S(1)}, u32[]{:S(2)}, u32[]{:S(2)}) collective-permute-start(bf16[4,64,512]{2,1,0:T(8,128)(2,1)S(1)} %get-tuple-element.16), channel_id=1, source_target_pairs={{0,3},{1,4},{2,5},{3,6},{4,7},{5,0},{6,1},{7,2},{8,11},{9,12},{10,... | collective-permute-start | bytes 786440 | tf_op jit(solution)/shard_map/ppermute | solution.py:147
  16.7 2.0 %collective-permute-start.3 = (bf16[4,64,512]{2,1,0:T(8,128)(2,1)S(1)}, bf16[4,64,512]{2,1,0:T(8,128)(2,1)S(1)}, u32[]{:S(2)}, u32[]{:S(2)}) collective-permute-start(bf16[4,64,512]{2,1,0:T(8,128)(2,1)S(1)} %get-tuple-element.16), channel_id=1, source_target_pairs={{0,4},{1,5},{2,6},{3,7},{4,0},{5,1},{6,2},{7,3},{8,12},{9,13},{10,... | collective-permute-start | bytes 786440 | tf_op jit(solution)/shard_map/ppermute | solution.py:147
  18.7 3.1 %collective-permute-start.4 = (bf16[4,64,512]{2,1,0:T(8,128)(2,1)S(1)}, bf16[4,64,512]{2,1,0:T(8,128)(2,1)S(1)}, u32[]{:S(2)}, u32[]{:S(2)}) collective-permute-start(bf16[4,64,512]{2,1,0:T(8,128)(2,1)S(1)} %get-tuple-element.16), channel_id=1, source_target_pairs={{0,5},{1,6},{2,7},{3,0},{4,1},{5,2},{6,3},{7,4},{8,13},{9,14},{10,... | collective-permute-start | bytes 786440 | tf_op jit(solution)/shard_map/ppermute | solution.py:147
  22.1 0.7 convert_element_type.36
  22.8 0.7 convert_element_type.39
  23.5 2.0 %select_reduce_fusion = (bf16[16,64,64]{2,1,0:T(8,128)(2,1)S(1)}, bf16[16,64,64]{2,1,0:T(8,128)(2,1)}) fusion(f32[16,9]{1,0:T(8,128)S(1)} %convert_element_type.39, pred[9,64,64]{2,1,0:T(8,128)(4,1)S(1)} %fusion.2, f32[16,9]{1,0:T(8,128)S(1)} %convert_element_type.36), kind=kLoop, calls=%fused_computation.1 | loop fusion | flops 2228224 | bytes 300160 | tf_op jit(solution)/shard_map/reduce_sum | solution.py:26
  25.6 0.9 copy.34
  26.5 1.3 broadcast_in_dim_reshape.6.bias_ref
  27.8 1.4 collective-permute-start.5
  29.3 1.0 constant_dynamic-update-slice_fusion.6
  30.2 1.1 collective-permute-start.6
  31.3 1.0 constant_dynamic-update-slice_fusion.5
  32.3 5.8 %collective-permute-done.2 = bf16[4,64,512]{2,1,0:T(8,128)(2,1)S(1)} collective-permute-done((bf16[4,64,512]{2,1,0:T(8,128)(2,1)S(1)}, bf16[4,64,512]{2,1,0:T(8,128)(2,1)S(1)}, u32[]{:S(2)}, u32[]{:S(2)}) %collective-permute-start.2) | collective-permute-done | bytes 262176 | tf_op jit(solution)/shard_map/ppermute | solution.py:147
  38.1 2.9 %collective-permute-done.4 = bf16[4,64,512]{2,1,0:T(8,128)(2,1)S(1)} collective-permute-done((bf16[4,64,512]{2,1,0:T(8,128)(2,1)S(1)}, bf16[4,64,512]{2,1,0:T(8,128)(2,1)S(1)}, u32[]{:S(2)}, u32[]{:S(2)}) %collective-permute-start.4) | collective-permute-done | bytes 262176 | tf_op jit(solution)/shard_map/ppermute | solution.py:147
  41.1 4.5 %collective-permute-done.6 = bf16[4,64,512]{2,1,0:T(8,128)(2,1)S(1)} collective-permute-done((bf16[4,64,512]{2,1,0:T(8,128)(2,1)S(1)}, bf16[4,64,512]{2,1,0:T(8,128)(2,1)S(1)}, u32[]{:S(2)}, u32[]{:S(2)}) %collective-permute-start.6) | collective-permute-done | bytes 262176 | tf_op jit(solution)/shard_map/ppermute | solution.py:147
  45.6 19.7 %all-gather.3.cloned.1.call-done = bf16[16,64,512]{2,1,0:T(8,128)(2,1)} async-done(((bf16[1,64,512]{2,1,0:T(8,128)(2,1)}), bf16[16,64,512]{2,1,0:T(8,128)(2,1)}) %all-gather.3.cloned.1.call-update) | async-done | bytes 1048592 | tf_op jit(solution)/shard_map/all_gather | solution.py:153
  65.3 42.1 %shard_map.64 = (f32[8,4,4,256]{3,2,1,0:T(4,128)}, f32[8,4,4,256]{3,2,1,0:T(4,128)}) custom-call(bf16[2048,512]{1,0:T(8,128)(2,1)} %bitcast.28, bf16[1024,512]{1,0:T(8,128)(2,1)} %bitcast.34, bf16[1024,64]{1,0:T(8,128)(2,1)} %bitcast.30, f32[1024,1]{1,0:T(8,128)} %broadcast_in_dim_reshape.6.bias_ref, bf16[16,64,64]{2,1,0:T(8,128)(2,1)} %bitcast.32), custom_call_target="tpu_custom_call" | custom-call | tf_op jit(solution)/shard_map/pallas_call | solution.py:105
  107.4 1.1 reshape.274
  108.5 0.3 reduce_sum.80
  108.7 0.2 copy.36
  108.9 1.1 reshape.275
  110.0 0.3 reduce_sum.82
  110.3 0.2 copy.37
  110.5 0.9 all-gather.5.cloned.1.call-done
  111.4 42.2 %shard_map.65 = (f32[8,4,4,256]{3,2,1,0:T(4,128)}, f32[8,4,4,256]{3,2,1,0:T(4,128)}) custom-call(bf16[2048,512]{1,0:T(8,128)(2,1)} %bitcast.29, bf16[1024,512]{1,0:T(8,128)(2,1)} %bitcast.35, bf16[1024,64]{1,0:T(8,128)(2,1)} %bitcast.31, f32[1024,1]{1,0:T(8,128)} %broadcast_in_dim_reshape.6.bias_ref, bf16[16,64,64]{2,1,0:T(8,128)(2,1)} %bitcast.33), custom_call_target="tpu_custom_call" | custom-call | tf_op jit(solution)/shard_map/pallas_call | solution.py:105
  153.6 1.1 reshape.277
  154.6 0.3 reduce_sum.83
  154.9 0.2 copy.39
  155.1 1.1 reshape.278
  156.2 0.3 reduce_sum.85
  156.4 0.2 copy.40
  156.7 0.6 gather_fusion
  157.4 0.7 reshape.288
  158.1 4.3 %all-to-all-start = ((f32[8,1,128]{2,1,0:T(1,128)}), f32[8,1,128]{2,1,0:T(1,128)S(1)}, u32[]{:S(2)}, u32[]{:S(2)}) async-start(f32[8,1,128]{2,1,0:T(1,128)} %reshape.288), calls=%async_computation | async-start | bytes 8192 | tf_op jit(solution)/shard_map/all_to_all | solution.py:158
  162.4 0.1 broadcast_in_dim.83
  162.5 5.9 %all-to-all-done = f32[8,1,128]{2,1,0:T(1,128)S(1)} async-done(((f32[8,1,128]{2,1,0:T(1,128)}), f32[8,1,128]{2,1,0:T(1,128)S(1)}, u32[]{:S(2)}, u32[]{:S(2)}) %all-to-all-start) | async-done | bytes 4128 | tf_op jit(solution)/shard_map/all_to_all | solution.py:158
  168.4 0.5 broadcast.348
  168.9 0.7 reduce
  169.7 0.2 copy.43
  169.9 0.1 broadcast_select_fusion
  170.0 0.7 copy.44
  (39 shorter events, 1.0 us)
Async XLA Ops:
  6.5 19.9 %copy-start.1 = (f32[16]{0:T(128)S(1)}, f32[16]{0:T(128)}, u32[]{:S(2)}) copy-start(f32[16]{0:T(128)} %param.10) | copy-start | bytes 196
  6.5 58.7 %all-gather.3.cloned.1.call-start = ((), (), s32[]{:S(2)}) async-start(), calls=%async_computation.1 | async-start | bytes 1114112 | tf_op jit(solution)/shard_map/all_gather | solution.py:153
  9.3 102.2 %all-gather.5.cloned.1.call-start = ((), (), s32[]{:S(2)}) async-start(), calls=%async_computation.2 | async-start | bytes 1114112 | tf_op jit(solution)/shard_map/all_gather | solution.py:153
  11.5 16.4 %collective-permute-start = (bf16[4,64,512]{2,1,0:T(8,128)(2,1)S(1)}, bf16[4,64,512]{2,1,0:T(8,128)(2,1)}, u32[]{:S(2)}, u32[]{:S(2)}) collective-permute-start(bf16[4,64,512]{2,1,0:T(8,128)(2,1)S(1)} %get-tuple-element.16), channel_id=1, source_target_pairs={{0,1},{1,2},{2,3},{3,4},{4,5},{5,6},{6,7},{7,0},{8,9},{9,10},{10,1... | collective-permute-start | bytes 786440 | tf_op jit(solution)/shard_map/ppermute | solution.py:147
  13.2 17.0 %collective-permute-start.1 = (bf16[4,64,512]{2,1,0:T(8,128)(2,1)S(1)}, bf16[4,64,512]{2,1,0:T(8,128)(2,1)}, u32[]{:S(2)}, u32[]{:S(2)}) collective-permute-start(bf16[4,64,512]{2,1,0:T(8,128)(2,1)S(1)} %get-tuple-element.16), channel_id=1, source_target_pairs={{0,2},{1,3},{2,4},{3,5},{4,6},{5,7},{6,0},{7,1},{8,10},{9,11},{10,... | collective-permute-start | bytes 786440 | tf_op jit(solution)/shard_map/ppermute | solution.py:147
  14.7 23.3 %collective-permute-start.2 = (bf16[4,64,512]{2,1,0:T(8,128)(2,1)S(1)}, bf16[4,64,512]{2,1,0:T(8,128)(2,1)S(1)}, u32[]{:S(2)}, u32[]{:S(2)}) collective-permute-start(bf16[4,64,512]{2,1,0:T(8,128)(2,1)S(1)} %get-tuple-element.16), channel_id=1, source_target_pairs={{0,3},{1,4},{2,5},{3,6},{4,7},{5,0},{6,1},{7,2},{8,11},{9,12},{10,... | collective-permute-start | bytes 786440 | tf_op jit(solution)/shard_map/ppermute | solution.py:147
  16.7 21.3 %collective-permute-start.3 = (bf16[4,64,512]{2,1,0:T(8,128)(2,1)S(1)}, bf16[4,64,512]{2,1,0:T(8,128)(2,1)S(1)}, u32[]{:S(2)}, u32[]{:S(2)}) collective-permute-start(bf16[4,64,512]{2,1,0:T(8,128)(2,1)S(1)} %get-tuple-element.16), channel_id=1, source_target_pairs={{0,4},{1,5},{2,6},{3,7},{4,0},{5,1},{6,2},{7,3},{8,12},{9,13},{10,... | collective-permute-start | bytes 786440 | tf_op jit(solution)/shard_map/ppermute | solution.py:147
  18.7 22.3 %collective-permute-start.4 = (bf16[4,64,512]{2,1,0:T(8,128)(2,1)S(1)}, bf16[4,64,512]{2,1,0:T(8,128)(2,1)S(1)}, u32[]{:S(2)}, u32[]{:S(2)}) collective-permute-start(bf16[4,64,512]{2,1,0:T(8,128)(2,1)S(1)} %get-tuple-element.16), channel_id=1, source_target_pairs={{0,5},{1,6},{2,7},{3,0},{4,1},{5,2},{6,3},{7,4},{8,13},{9,14},{10,... | collective-permute-start | bytes 786440 | tf_op jit(solution)/shard_map/ppermute | solution.py:147
  27.8 13.2 %collective-permute-start.5 = (bf16[4,64,512]{2,1,0:T(8,128)(2,1)S(1)}, bf16[4,64,512]{2,1,0:T(8,128)(2,1)S(1)}, u32[]{:S(2)}, u32[]{:S(2)}) collective-permute-start(bf16[4,64,512]{2,1,0:T(8,128)(2,1)S(1)} %get-tuple-element.16), channel_id=1, source_target_pairs={{0,6},{1,7},{2,0},{3,1},{4,2},{5,3},{6,4},{7,5},{8,14},{9,15},{10,... | collective-permute-start | bytes 786440 | tf_op jit(solution)/shard_map/ppermute | solution.py:147
  30.2 15.3 %collective-permute-start.6 = (bf16[4,64,512]{2,1,0:T(8,128)(2,1)S(1)}, bf16[4,64,512]{2,1,0:T(8,128)(2,1)S(1)}, u32[]{:S(2)}, u32[]{:S(2)}) collective-permute-start(bf16[4,64,512]{2,1,0:T(8,128)(2,1)S(1)} %get-tuple-element.16), channel_id=1, source_target_pairs={{0,7},{1,0},{2,1},{3,2},{4,3},{5,4},{6,5},{7,6},{8,15},{9,8},{10,9... | collective-permute-start | bytes 786440 | tf_op jit(solution)/shard_map/ppermute | solution.py:147
  45.6 19.7 %copy-start = (bf16[32,64,512]{2,1,0:T(8,128)(2,1)}, bf16[32,64,512]{2,1,0:T(8,128)(2,1)S(1)}, u32[]{:S(2)}) copy-start(bf16[32,64,512]{2,1,0:T(8,128)(2,1)S(1)} %constant_dynamic-update-slice_fusion) | copy-start | bytes 6291460
  153.6 8.8 %copy-start.2 = (s32[1,16]{1,0:T(1,128)S(1)}, s32[1,16]{1,0:T(1,128)}, u32[]{:S(2)}) copy-start(s32[1,16]{1,0:T(1,128)} %param.11) | copy-start | bytes 196
  158.1 10.4 %all-to-all-start = ((f32[8,1,128]{2,1,0:T(1,128)}), f32[8,1,128]{2,1,0:T(1,128)S(1)}, u32[]{:S(2)}, u32[]{:S(2)}) async-start(f32[8,1,128]{2,1,0:T(1,128)} %reshape.288), calls=%async_computation | async-start | bytes 8192 | tf_op jit(solution)/shard_map/all_to_all | solution.py:158
Sparse Core Ops, SparseCore 0:
  9.8 55.4 all-gather.2
  67.7 43.6 all-gather.4

commit v5 on v4

v5 whole, which is shorter than its diff:
```python
import math

import jax
import jax.numpy as jnp
from jax import lax
from jax.experimental import pallas as pl
from jax.experimental.pallas import tpu as pltpu
from jax.sharding import PartitionSpec as P

SIDE = 8


epsilon = 1e-06


def conv_table(weights, width):
    count = width * width
    position = jnp.arange(count, dtype=jnp.int32)
    grid_row = position // width
    grid_col = position % width
    delta_row = grid_row[None, :] - grid_row[:, None]
    delta_col = grid_col[None, :] - grid_col[:, None]
    inside = (jnp.abs(delta_row) <= 1) & (jnp.abs(delta_col) <= 1)
    tap_index = (delta_row + 1) * 3 + (delta_col + 1)
    selector = (tap_index[None] == jnp.arange(9, dtype=jnp.int32)[:, None, None]) & inside[None]
    table = jnp.sum(
        jnp.where(selector[None], weights.astype(jnp.float32)[:, :, None, None], jnp.float32(0.0)),
        axis=1,
    )
    return table.astype(jnp.bfloat16)


def normalize(features):
    values = features.astype(jnp.float32)
    inverse_rms = lax.rsqrt(jnp.mean(values * values, axis=-1, keepdims=True) + epsilon)
    return (values * inverse_rms).astype(jnp.bfloat16)


CH = 256


GB = 4


def filter_kernel(idx_ref, cnt_ref, q_ref, r_ref, qt_ref, bias_ref, rtt_ref, col_ref, row_ref,
                  c_scr, h_scr, rt_ref, f_scr):
    t = pl.program_id(0)
    rows = q_ref.shape[0]
    hid = rtt_ref.shape[0]
    cells = rtt_ref.shape[1]
    depth = q_ref.shape[1]
    nq = rows // cells
    r4 = CH // cells
    br = r4 // 2
    groups = col_ref.shape[2] // 2
    scale = math.sqrt(depth)
    per = hid // 4

    @pl.when(t == 0)
    def _():
        rt_ref[...] = jnp.zeros(rt_ref.shape, rt_ref.dtype)
        for k in range(hid):
            blockk = rtt_ref[k]
            for x in range(r4):
                rt_ref[k, x * cells:(x + 1) * cells, x * cells:(x + 1) * cells] = blockk

    qt = q_ref[...]
    for g in range(groups):
        @pl.when(g * GB < cnt_ref[t])
        def _():
            for slot in range(GB):
                blk_id = idx_ref[t, g * GB + slot]
                start = pl.multiple_of(blk_id * (br * cells), br * cells)
                corr = lax.dot_general(
                    qt, r_ref[pl.ds(start, br * cells), :], (((1,), (1,)), ((), ())),
                    preferred_element_type=jnp.float32,
                )
                c_scr[:, slot * br * cells:(slot + 1) * br * cells] = (corr / scale).astype(jnp.bfloat16)
            for p in range(nq):
                for c2 in range(2):
                    cc = c_scr[p * cells:(p + 1) * cells, c2 * CH:(c2 + 1) * CH]
                    for kg in range(hid // per):
                        hq = jnp.dot(
                            qt_ref[kg * per * cells:(kg + 1) * per * cells, :], cc,
                            preferred_element_type=jnp.float32,
                        )
                        hq = jnp.maximum(hq + bias_ref[kg * per * cells:(kg + 1) * per * cells, :], 0.0)
                        hq = hq.astype(jnp.bfloat16)
                        for kk in range(per):
                            k = kg * per + kk
                            row0 = (p * 2 + c2) * cells
                            h_scr[k, row0:row0 + cells, :] = hq[kk * cells:(kk + 1) * cells, :]
            f_scr[...] = jnp.dot(h_scr[0], rt_ref[0], preferred_element_type=jnp.float32)
            for k in range(1, hid):
                f_scr[...] += jnp.dot(h_scr[k], rt_ref[k], preferred_element_type=jnp.float32)
            for p in range(nq):
                acc = f_scr[p * 2 * cells:(p + 1) * 2 * cells, :]
                col_ref[0, p, 2 * g:2 * g + 2, :] = jnp.max(acc.reshape(2, cells, CH), axis=1)
                accT = acc.T
                row_ref[0, p, :, 2 * g * cells:(2 * g + 2) * cells] = jnp.max(
                    accT.reshape(r4, cells, 2 * cells), axis=1)


def local_scores(q_all, r_all, cand, query_table, ref_table, tap_bias):
    nql, cells, depth = q_all.shape
    nrl = r_all.shape[0]
    hid = query_table.shape[0]
    qt_per = 4
    tiles = nql // qt_per
    nb = cand.shape[1]
    br = nrl // nb
    chunks = nrl * cells // CH
    r4 = CH // cells
    keep = (cand != 0).astype(jnp.int32)
    idx = jnp.argsort(1 - keep, axis=1, stable=True).astype(jnp.int32)
    cnt = jnp.sum(keep, axis=1).astype(jnp.int32)
    qstack = query_table.reshape(hid * cells, cells)
    bias_col = jnp.repeat(tap_bias.astype(jnp.float32), cells)[:, None]
    rtT = jnp.transpose(ref_table, (0, 2, 1))
    q2 = q_all.reshape(nql * cells, depth)
    r2 = r_all.reshape(nrl * cells, depth)
    col, row = pl.pallas_call(
        filter_kernel,
        grid_spec=pltpu.PrefetchScalarGridSpec(
            num_scalar_prefetch=2,
            grid=(tiles,),
            in_specs=[
                pl.BlockSpec((qt_per * cells, depth), lambda t, i, c: (t, 0)),
                pl.BlockSpec((nrl * cells, depth), lambda t, i, c: (0, 0)),
                pl.BlockSpec((hid * cells, cells), lambda t, i, c: (0, 0)),
                pl.BlockSpec((hid * cells, 1), lambda t, i, c: (0, 0)),
                pl.BlockSpec((hid, cells, cells), lambda t, i, c: (0, 0, 0)),
            ],
            out_specs=[
                pl.BlockSpec((1, qt_per, chunks, CH), lambda t, i, c: (t, 0, 0, 0)),
                pl.BlockSpec((1, qt_per, r4, chunks * cells), lambda t, i, c: (t, 0, 0, 0)),
            ],
            scratch_shapes=[
                pltpu.VMEM((qt_per * cells, GB * br * cells), jnp.bfloat16),
                pltpu.VMEM((hid, qt_per * 2 * cells, CH), jnp.bfloat16),
                pltpu.VMEM((hid, CH, CH), jnp.bfloat16),
                pltpu.VMEM((qt_per * 2 * cells, CH), jnp.float32),
            ],
        ),
        out_shape=[
            jax.ShapeDtypeStruct((tiles, qt_per, chunks, CH), jnp.float32),
            jax.ShapeDtypeStruct((tiles, qt_per, r4, chunks * cells), jnp.float32),
        ],
        compiler_params=pltpu.CompilerParams(vmem_limit_bytes=56 * 1024 * 1024),
    )(idx, cnt, q2, r2, qstack, bias_col, rtT)
    col_pool = jnp.mean(col.reshape(tiles, qt_per, chunks, r4, cells), axis=-1)
    row_pool = jnp.mean(row.reshape(tiles, qt_per, r4, chunks, cells), axis=-1)
    row_pool = jnp.transpose(row_pool, (0, 1, 3, 2))
    packed = (0.5 * (row_pool + col_pool)).reshape(tiles, qt_per, nb, br)
    where_is = jnp.argsort(idx, axis=1)
    return jnp.take_along_axis(packed, where_is[:, None, :, None], axis=2)


def shards(queries, references, query_taps, ref_taps, tap_bias, candidates):
    query_table = conv_table(query_taps, SIDE)
    ref_table = conv_table(ref_taps, SIDE)
    query_unit = normalize(queries)
    ref_unit = normalize(references)
    blk = lax.axis_size("blk")
    wide = lax.axis_size("wide")
    qt_per = query_unit.shape[0]
    rl = ref_unit.shape[0]
    me = lax.axis_index("blk")
    payload = jnp.concatenate(
        [query_unit.reshape(-1), candidates.reshape(-1).astype(jnp.bfloat16)])
    pieces = [payload] + [
        lax.ppermute(payload, "blk", [(i, (i + d) % blk) for i in range(blk)])
        for d in range(1, blk)
    ]
    qsize = query_unit.size
    q_all = jnp.concatenate([x[:qsize] for x in pieces]).reshape(
        (blk * qt_per,) + query_unit.shape[1:])
    cand = jnp.stack([x[qsize:] for x in pieces])
    r_all = lax.all_gather(ref_unit, "wide", axis=0, tiled=True)
    s = local_scores(q_all, r_all, cand, query_table, ref_table, tap_bias)
    outgoing = jnp.take(s, (me - jnp.arange(blk)) % blk, axis=0)
    mine = lax.all_to_all(outgoing, "blk", 0, 0, tiled=True)
    mine = jnp.transpose(mine, (1, 2, 0, 3)).reshape(qt_per, wide * blk * rl)
    block_refs = blk * rl
    keep = jnp.repeat(candidates[0] != 0, block_refs)
    return jnp.where(keep[None, :], mine, jnp.float32(0.0))


def solution(mesh):
    placed = (
        P(("wide", "blk"), None, None),
        P(("wide", "blk"), None, None),
        P(),
        P(),
        P(),
        P(("wide", "blk"), None),
    )
    return jax.shard_map(
        shards, mesh=mesh, in_specs=placed, out_specs=P(("wide", "blk"), None), check_vma=False
    )
```

time: 178 us -> 167 us (0.938)
  the two profiles are of different devices: /device:TPU:0 before, /device:TPU:1 now
where the time goes in v5:
time: 167 us; the launch traced here: 166 us
  Pallas kernels  61.3 us (37%)
  waiting for transfers between devices  37.3 us (22%)
  local copies, waits for them, and re-layouts  27.2 us (16%)
  starting transfers between devices  16.1 us (10%)
  between operations  13.8 us (8%)
  other arithmetic  9.92 us (6%)
    pallas_call x1, Pallas kernels, local_scores(): pl.pallas_call(filter_kernel, grid_spec=pltpu.PrefetchScalarGridSpec(num_...  61.3 us
    all_gather x1, waiting for transfers between devices, shards(): r_all = lax.all_gather(ref_unit, 'wide', axis=0, tiled=True)  16.8 us
    ppermute x7, waiting for transfers between devices, shards(): lax.ppermute(payload, 'blk', [(i, (i + d) % blk) for i in range(blk)])  15.7 us
    ppermute x7, starting transfers between devices, shards(): lax.ppermute(payload, 'blk', [(i, (i + d) % blk) for i in range(blk)])  12 us
    slice x7, local copies, waits for them, and re-layouts, shards(): x[:qsize]  7.01 us
    concatenate x8, local copies, waits for them, and re-layouts, shards(): jnp.concatenate([x[:qsize] for x in pieces])  5.44 us
    all_to_all x1, waiting for transfers between devices, shards(): mine = lax.all_to_all(outgoing, 'blk', 0, 0, tiled=True)  4.77 us
    all_to_all x1, starting transfers between devices, shards(): mine = lax.all_to_all(outgoing, 'blk', 0, 0, tiled=True)  4 us
  transfers between devices with their start and end apart: 9, of which 5 were waited for; matrix products, arithmetic and copies ran while one was open for 15% of the time, Pallas kernels for 0%

profile of v5, /device:TPU:1, one launch (start us, length us, event | category | flops | bytes accessed | tf_op | source)
XLA Modules:
  0.0 165.6 jit_solution(14476540040081149467)
XLA Ops:
  6.6 1.1 fusion
  7.7 1.1 fusion.1
  8.9 0.7 copy.76
  9.8 2.2 %collective-permute-start = (bf16[131088]{0:T(1024)(128)(2,1)S(1)}, bf16[131088]{0:T(1024)(128)(2,1)S(1)}, u32[]{:S(2)}, u32[]{:S(2)}) collective-permute-start(bf16[131088]{0:T(1024)(128)(2,1)S(1)} %pad_maximum_fusion), channel_id=1, source_target_pairs={{0,1},{1,2},{2,3},{3,4},{4,5},{5,6},{6,7},{7,0},{8,9},{9,10},{10,1... | collective-permute-start | bytes 786536 | tf_op jit(solution)/shard_map/ppermute | solution.py:172
  12.0 1.2 collective-permute-start.1
  13.2 1.7 %collective-permute-start.2 = (bf16[131088]{0:T(1024)(128)(2,1)S(1)}, bf16[131088]{0:T(1024)(128)(2,1)}, u32[]{:S(2)}, u32[]{:S(2)}) collective-permute-start(bf16[131088]{0:T(1024)(128)(2,1)S(1)} %pad_maximum_fusion), channel_id=1, source_target_pairs={{0,3},{1,4},{2,5},{3,6},{4,7},{5,0},{6,1},{7,2},{8,11},{9,12},{10,... | collective-permute-start | bytes 786536 | tf_op jit(solution)/shard_map/ppermute | solution.py:172
  14.9 1.7 %collective-permute-start.3 = (bf16[131088]{0:T(1024)(128)(2,1)S(1)}, bf16[131088]{0:T(1024)(128)(2,1)}, u32[]{:S(2)}, u32[]{:S(2)}) collective-permute-start(bf16[131088]{0:T(1024)(128)(2,1)S(1)} %pad_maximum_fusion), channel_id=1, source_target_pairs={{0,4},{1,5},{2,6},{3,7},{4,0},{5,1},{6,2},{7,3},{8,12},{9,13},{10,... | collective-permute-start | bytes 786536 | tf_op jit(solution)/shard_map/ppermute | solution.py:172
  16.7 2.9 %collective-permute-start.4 = (bf16[131088]{0:T(1024)(128)(2,1)S(1)}, bf16[131088]{0:T(1024)(128)(2,1)}, u32[]{:S(2)}, u32[]{:S(2)}) collective-permute-start(bf16[131088]{0:T(1024)(128)(2,1)S(1)} %pad_maximum_fusion), channel_id=1, source_target_pairs={{0,5},{1,6},{2,7},{3,0},{4,1},{5,2},{6,3},{7,4},{8,13},{9,14},{10,... | collective-permute-start | bytes 786536 | tf_op jit(solution)/shard_map/ppermute | solution.py:172
  19.5 1.0 fusion.3
  20.5 0.7 fusion.4
  21.6 2.0 %select_reduce_fusion = (bf16[16,64,64]{2,1,0:T(8,128)(2,1)S(1)}, bf16[16,64,64]{2,1,0:T(8,128)(2,1)}) fusion(f32[16,9]{1,0:T(8,128)S(1)} %convert_element_type.52, pred[9,64,64]{2,1,0:T(8,128)(4,1)S(1)} %fusion.2, f32[16,9]{1,0:T(8,128)S(1)} %convert_element_type.49), kind=kLoop, calls=%fused_computation.2 | loop fusion | flops 2228224 | bytes 300160 | tf_op jit(solution)/shard_map/reduce_sum | solution.py:26
  23.7 0.9 copy.85
  24.6 1.3 broadcast_in_dim_reshape.5.bias_ref
  25.9 1.2 collective-permute-start.5
  27.1 1.1 collective-permute-start.6
  28.2 7.1 %collective-permute-done.2 = bf16[131088]{0:T(1024)(128)(2,1)} collective-permute-done((bf16[131088]{0:T(1024)(128)(2,1)S(1)}, bf16[131088]{0:T(1024)(128)(2,1)}, u32[]{:S(2)}, u32[]{:S(2)}) %collective-permute-start.2) | collective-permute-done | bytes 262208 | tf_op jit(solution)/shard_map/ppermute | solution.py:172
  35.3 0.7 slice_bitcast_fusion.4
  36.0 0.7 slice_bitcast_fusion.3
  36.7 1.0 collective-permute-done.4
  37.7 0.7 slice_bitcast_fusion.2
  38.9 7.6 %collective-permute-done.6 = bf16[131088]{0:T(1024)(128)(2,1)S(1)} collective-permute-done((bf16[131088]{0:T(1024)(128)(2,1)S(1)}, bf16[131088]{0:T(1024)(128)(2,1)S(1)}, u32[]{:S(2)}, u32[]{:S(2)}) %collective-permute-start.6) | collective-permute-done | bytes 262208 | tf_op jit(solution)/shard_map/ppermute | solution.py:172
  46.7 0.6 convert_reduce_fusion
  47.4 0.7 sort.34
  48.1 0.7 copy.86.idx_ref
  49.1 1.0 slice.69
  50.3 1.0 slice.70
  51.4 1.7 %slice.71 = bf16[131072]{0:T(1024)(128)(2,1)} slice(bf16[131088]{0:T(1024)(128)(2,1)} %collective-permute-done.4), slice={[0:131072]} | slice | bytes 524288 | tf_op jit(solution)/shard_map/slice | solution.py:176
  53.1 1.1 concatenate.29
  54.2 1.7 %slice.72 = bf16[131072]{0:T(1024)(128)(2,1)} slice(bf16[131088]{0:T(1024)(128)(2,1)} %copy-done.4), slice={[0:131072]} | slice | bytes 524288 | tf_op jit(solution)/shard_map/slice | solution.py:176
  55.9 1.8 %concatenate.30 = bf16[256,512]{1,0:T(8,128)(2,1)} reshape(bf16[131072]{0:T(1024)(128)(2,1)} %slice.72) | data formatting | bytes 524288 | tf_op jit(solution)/shard_map/concatenate | solution.py:176
  57.7 1.7 %slice.73 = bf16[131072]{0:T(1024)(128)(2,1)} slice(bf16[131088]{0:T(1024)(128)(2,1)} %copy-done.5), slice={[0:131072]} | slice | bytes 524288 | tf_op jit(solution)/shard_map/slice | solution.py:176
  59.4 1.8 %concatenate.31 = bf16[256,512]{1,0:T(8,128)(2,1)} reshape(bf16[131072]{0:T(1024)(128)(2,1)} %slice.73) | data formatting | bytes 524288 | tf_op jit(solution)/shard_map/concatenate | solution.py:176
  61.2 0.7 sort.35
  62.3 0.8 copy-done.1
  63.3 16.8 %all-gather.2.cloned.1.call-done = bf16[32,64,512]{2,1,0:T(8,128)(2,1)} async-done(((bf16[2,64,512]{2,1,0:T(8,128)(2,1)}), bf16[32,64,512]{2,1,0:T(8,128)(2,1)}) %all-gather.2.cloned.1.call-update) | async-done | bytes 2097168 | tf_op jit(solution)/shard_map/all_gather | solution.py:179
  80.1 61.3 %shard_map.64 = (f32[8,4,8,256]{3,2,1,0:T(8,128)}, f32[8,4,4,512]{3,2,1,0:T(4,128)}) custom-call(s32[8,16]{1,0:T(8,128)} %copy.86.idx_ref, s32[8]{0:T(128)} %get-tuple-element.17.cnt_ref, bf16[2048,512]{1,0:T(8,128)(2,1)} %copy-done, bf16[2048,512]{1,0:T(8,128)(2,1)} %bitcast.49, bf16[1024,64]{1,0:T(8,128)(2,1)} %bitcast.51, ...), custom_call_target="tpu_custom_call" | custom-call | tf_op jit(solution)/shard_map/pallas_call | solution.py:122
  141.4 1.2 reshape.293
  142.5 0.3 reduce_sum.72
  143.1 1.2 reshape.292
  144.7 0.3 copy.92
  145.0 0.9 gather_fusion.1
  146.1 0.6 gather_fusion
  146.8 0.7 reshape.317
  147.5 4.0 %all-to-all-start = ((f32[8,1,128]{2,1,0:T(1,128)}), f32[8,1,128]{2,1,0:T(1,128)S(1)}, u32[]{:S(2)}, u32[]{:S(2)}) async-start(f32[8,1,128]{2,1,0:T(1,128)} %reshape.317), calls=%async_computation | async-start | bytes 8192 | tf_op jit(solution)/shard_map/all_to_all | solution.py:182
  151.7 4.8 %all-to-all-done = f32[8,1,128]{2,1,0:T(1,128)S(1)} async-done(((f32[8,1,128]{2,1,0:T(1,128)}), f32[8,1,128]{2,1,0:T(1,128)S(1)}, u32[]{:S(2)}, u32[]{:S(2)}) %all-to-all-start) | async-done | bytes 4128 | tf_op jit(solution)/shard_map/all_to_all | solution.py:182
  156.4 0.5 broadcast.378
  157.0 0.7 reduce.2
  158.0 0.7 copy.95
  (88 shorter events, 4.1 us)
Async XLA Ops:
  6.5 14.0 %copy-start.3 = (bf16[2,64,512]{2,1,0:T(8,128)(2,1)S(1)}, bf16[2,64,512]{2,1,0:T(8,128)(2,1)}, u32[]{:S(2)}) copy-start(bf16[2,64,512]{2,1,0:T(8,128)(2,1)} %param.7) | copy-start | bytes 393220
  6.5 15.0 %copy-start.6 = (bf16[16,9]{1,0:T(8,128)(2,1)S(1)}, bf16[16,9]{1,0:T(8,128)(2,1)}, u32[]{:S(2)}) copy-start(bf16[16,9]{1,0:T(8,128)(2,1)} %param.8) | copy-start | bytes 868
  6.5 15.1 %copy-start.7 = (bf16[16,9]{1,0:T(8,128)(2,1)S(1)}, bf16[16,9]{1,0:T(8,128)(2,1)}, u32[]{:S(2)}) copy-start(bf16[16,9]{1,0:T(8,128)(2,1)} %param.9) | copy-start | bytes 868
  6.5 18.0 %copy-start.8 = (f32[16]{0:T(128)S(1)}, f32[16]{0:T(128)}, u32[]{:S(2)}) copy-start(f32[16]{0:T(128)} %param.10) | copy-start | bytes 196
  6.5 73.5 %all-gather.2.cloned.1.call-start = ((), (), s32[]{:S(2)}) async-start(), calls=%async_computation.1 | async-start | bytes 2228224 | tf_op jit(solution)/shard_map/all_gather | solution.py:179
  9.8 16.1 %collective-permute-start = (bf16[131088]{0:T(1024)(128)(2,1)S(1)}, bf16[131088]{0:T(1024)(128)(2,1)S(1)}, u32[]{:S(2)}, u32[]{:S(2)}) collective-permute-start(bf16[131088]{0:T(1024)(128)(2,1)S(1)} %pad_maximum_fusion), channel_id=1, source_target_pairs={{0,1},{1,2},{2,3},{3,4},{4,5},{5,6},{6,7},{7,0},{8,9},{9,10},{10,1... | collective-permute-start | bytes 786536 | tf_op jit(solution)/shard_map/ppermute | solution.py:172
  12.0 15.1 %collective-permute-start.1 = (bf16[131088]{0:T(1024)(128)(2,1)S(1)}, bf16[131088]{0:T(1024)(128)(2,1)S(1)}, u32[]{:S(2)}, u32[]{:S(2)}) collective-permute-start(bf16[131088]{0:T(1024)(128)(2,1)S(1)} %pad_maximum_fusion), channel_id=1, source_target_pairs={{0,2},{1,3},{2,4},{3,5},{4,6},{5,7},{6,0},{7,1},{8,10},{9,11},{10,... | collective-permute-start | bytes 786536 | tf_op jit(solution)/shard_map/ppermute | solution.py:172
  13.2 22.1 %collective-permute-start.2 = (bf16[131088]{0:T(1024)(128)(2,1)S(1)}, bf16[131088]{0:T(1024)(128)(2,1)}, u32[]{:S(2)}, u32[]{:S(2)}) collective-permute-start(bf16[131088]{0:T(1024)(128)(2,1)S(1)} %pad_maximum_fusion), channel_id=1, source_target_pairs={{0,3},{1,4},{2,5},{3,6},{4,7},{5,0},{6,1},{7,2},{8,11},{9,12},{10,... | collective-permute-start | bytes 786536 | tf_op jit(solution)/shard_map/ppermute | solution.py:172
  14.9 21.1 %collective-permute-start.3 = (bf16[131088]{0:T(1024)(128)(2,1)S(1)}, bf16[131088]{0:T(1024)(128)(2,1)}, u32[]{:S(2)}, u32[]{:S(2)}) collective-permute-start(bf16[131088]{0:T(1024)(128)(2,1)S(1)} %pad_maximum_fusion), channel_id=1, source_target_pairs={{0,4},{1,5},{2,6},{3,7},{4,0},{5,1},{6,2},{7,3},{8,12},{9,13},{10,... | collective-permute-start | bytes 786536 | tf_op jit(solution)/shard_map/ppermute | solution.py:172
  16.7 21.0 %collective-permute-start.4 = (bf16[131088]{0:T(1024)(128)(2,1)S(1)}, bf16[131088]{0:T(1024)(128)(2,1)}, u32[]{:S(2)}, u32[]{:S(2)}) collective-permute-start(bf16[131088]{0:T(1024)(128)(2,1)S(1)} %pad_maximum_fusion), channel_id=1, source_target_pairs={{0,5},{1,6},{2,7},{3,0},{4,1},{5,2},{6,3},{7,4},{8,13},{9,14},{10,... | collective-permute-start | bytes 786536 | tf_op jit(solution)/shard_map/ppermute | solution.py:172
  25.9 12.9 %collective-permute-start.5 = (bf16[131088]{0:T(1024)(128)(2,1)S(1)}, bf16[131088]{0:T(1024)(128)(2,1)S(1)}, u32[]{:S(2)}, u32[]{:S(2)}) collective-permute-start(bf16[131088]{0:T(1024)(128)(2,1)S(1)} %pad_maximum_fusion), channel_id=1, source_target_pairs={{0,6},{1,7},{2,0},{3,1},{4,2},{5,3},{6,4},{7,5},{8,14},{9,15},{10,... | collective-permute-start | bytes 786536 | tf_op jit(solution)/shard_map/ppermute | solution.py:172
  27.1 19.5 %collective-permute-start.6 = (bf16[131088]{0:T(1024)(128)(2,1)S(1)}, bf16[131088]{0:T(1024)(128)(2,1)S(1)}, u32[]{:S(2)}, u32[]{:S(2)}) collective-permute-start(bf16[131088]{0:T(1024)(128)(2,1)S(1)} %pad_maximum_fusion), channel_id=1, source_target_pairs={{0,7},{1,0},{2,1},{3,2},{4,3},{5,4},{6,5},{7,6},{8,15},{9,8},{10,9... | collective-permute-start | bytes 786536 | tf_op jit(solution)/shard_map/ppermute | solution.py:172
  38.8 10.1 %copy-start.4 = (bf16[131088]{0:T(1024)(128)(2,1)}, bf16[131088]{0:T(1024)(128)(2,1)S(1)}, u32[]{:S(2)}) copy-start(bf16[131088]{0:T(1024)(128)(2,1)S(1)} %collective-permute-done.5) | copy-start | bytes 786532
  46.5 3.6 %copy-start.5 = (bf16[131088]{0:T(1024)(128)(2,1)}, bf16[131088]{0:T(1024)(128)(2,1)S(1)}, u32[]{:S(2)}) copy-start(bf16[131088]{0:T(1024)(128)(2,1)S(1)} %collective-permute-done.6) | copy-start | bytes 786532
  62.2 1.0 copy-start.1
  62.2 1.0 copy-start.2
  63.2 16.8 %copy-start = (bf16[2048,512]{1,0:T(8,128)(2,1)}, bf16[2048,512]{1,0:T(8,128)(2,1)S(1)}, u32[]{:S(2)}) copy-start(bf16[2048,512]{1,0:T(8,128)(2,1)S(1)} %constant_dynamic-update-slice_fusion.q_ref) | copy-start | bytes 6291460
  142.5 9.0 %copy-start.9 = (s32[1,16]{1,0:T(1,128)S(1)}, s32[1,16]{1,0:T(1,128)}, u32[]{:S(2)}) copy-start(s32[1,16]{1,0:T(1,128)} %param.11) | copy-start | bytes 196
  147.5 9.0 %all-to-all-start = ((f32[8,1,128]{2,1,0:T(1,128)}), f32[8,1,128]{2,1,0:T(1,128)S(1)}, u32[]{:S(2)}, u32[]{:S(2)}) async-start(f32[8,1,128]{2,1,0:T(1,128)} %reshape.317), calls=%async_computation | async-start | bytes 8192 | tf_op jit(solution)/shard_map/all_to_all | solution.py:182
Sparse Core Ops, SparseCore 0:
  21.4 58.6 all-gather.1
